TPU v7x, 32 devices: a whole 2x2x4 slice. The times are simulated.
32 devices in a mesh: segment: 4 (over z), dp: 8 (over y, x, core).
Axes of the slice: x: 2, y: 2, z: 4, core: 2. Of those that a mesh axis runs over, the one named last changes fastest.
Arguments:
- x_in: bfloat16 [2, 512, 8192], P(None, 'dp'), may hold values from -6 to 6
- cotangent: bfloat16 [2, 512, 8192], P(None, 'dp'), may hold values from -6 to 6
- weights: bfloat16 [1024, 128, 128], P('segment'), may hold values from -0.375 to 0.375
- block_index: int32 [1024, 3], P('segment'), may hold values from 0 to 63, as said below
Outputs:
- weight_grad: float32 [1024, 128, 128], P(('segment', 'dp'))
Inputs may be any that keep to these rules, and one draw needn't show every extreme that they name: `block_index`: within each segment's 2 * 128 rows, layer slot j takes rows j * 128 to (j + 1) * 128 - 1. A segment holds 1 to 2 layers, the first ones; the rest have all flags 0; some segment holds 2. A held layer has 32 to 128 kept slots, flags 1 first; some layer keeps 128. The (row, column) pairs of one layer's slots are distinct. Rows and columns of empty slots are arbitrary.
All inputs are finite; a program needn't handle non-finite values.
Results may differ from a plain program's by a relative error of at most 0.013.
Values may be sent and summed in bfloat16 or wider, within the bound.
No kernel may reach another device: no remote copies, remote signals or barrier semaphores. Data moves between devices by JAX's collectives and lax.ppermute only.
A program may use at most 192 MiB of HBM per device.

v0:
```python
import functools

import jax
import jax.numpy as jnp
from jax import lax
from jax.experimental import pallas as pl
from jax.experimental.pallas import tpu as pltpu
from jax.sharding import PartitionSpec as P

BLK = 128
LSLOT = 2
KMAX = 128
CH = 512
NSUB = 16
VMEM_LIMIT = 60 * 1024 * 1024

_SMEM = pl.BlockSpec(memory_space=pltpu.SMEM)
_VMEM = pl.BlockSpec(memory_space=pltpu.VMEM)
_ANY = pl.BlockSpec(memory_space=pl.ANY)


def shifted(value, axis, steps):
    count = lax.axis_size(axis)
    leading, last = (max(0, -steps), min(count, count - steps))
    return lax.ppermute(value, axis, [(source, source + steps) for source in range(leading, last)])


def _blk(i):
    return pl.ds(pl.multiple_of(i * BLK, BLK), BLK)


def _chunk(j):
    return pl.ds(pl.multiple_of(j * CH, CH), CH)


def _flag(idx_ref, k):
    return jnp.where(idx_ref[3 * k + 2] > 0, 1.0, 0.0).astype(jnp.float32)


def _w_copies(w_hbm, base, w_vmem, sems):
    copies = []
    for j in range(w_vmem.shape[0] // NSUB):
        copy = pltpu.make_async_copy(
            w_hbm.at[pl.ds(base + j * NSUB, NSUB)], w_vmem.at[pl.ds(j * NSUB, NSUB)], sems.at[j]
        )
        copy.start()
        copies.append(copy)
    return copies


def _slot_chunks(idx_ref, copies, body):
    for j, copy in enumerate(copies):
        copy.wait()

        @pl.when(idx_ref[3 * j * NSUB + 2] > 0)
        def _():
            for k in range(j * NSUB, (j + 1) * NSUB):
                body(k)


def _fwd_kernel(base, idx_ref, h_ref, w_hbm, hout_ref, y_ref, w_vmem, sems):
    width = h_ref.shape[1]
    copies = _w_copies(w_hbm, base, w_vmem, sems)
    y_ref[...] = jnp.zeros_like(y_ref)

    def body(k):
        r = idx_ref[3 * k]
        c = idx_ref[3 * k + 1]
        p = jnp.dot(h_ref[:, _blk(r)], w_vmem[k], preferred_element_type=jnp.float32)
        y_ref[:, _blk(c)] += p * _flag(idx_ref, k)

    _slot_chunks(idx_ref, copies, body)

    def epi(j, carry):
        y = y_ref[:, _chunk(j)]
        h = h_ref[:, _chunk(j)].astype(jnp.float32)
        hout_ref[:, _chunk(j)] = (h + y / (1.0 + jnp.exp(-y))).astype(hout_ref.dtype)
        return carry

    lax.fori_loop(0, width // CH, epi, 0)


def layer_forward(h, weights, layer, il):
    rows, width = h.shape
    return pl.pallas_call(
        functools.partial(_fwd_kernel, layer * KMAX),
        out_shape=(
            jax.ShapeDtypeStruct((rows, width), jnp.bfloat16),
            jax.ShapeDtypeStruct((rows, width), jnp.float32),
        ),
        in_specs=[_SMEM, _VMEM, _ANY],
        out_specs=(_VMEM, _VMEM),
        scratch_shapes=[
            pltpu.VMEM((KMAX, BLK, BLK), weights.dtype),
            pltpu.SemaphoreType.DMA((KMAX // NSUB,)),
        ],
        compiler_params=pltpu.CompilerParams(vmem_limit_bytes=VMEM_LIMIT),
    )(il.reshape(-1), h, weights)


def _bwd_kernel(base, idx_ref, g_ref, y_ref, w_hbm, gout_ref, s_ref, sp_ref, w_vmem, sems):
    width = g_ref.shape[1]
    copies = _w_copies(w_hbm, base, w_vmem, sems)

    def pre(j, carry):
        y = y_ref[:, _chunk(j)]
        sig = 1.0 / (1.0 + jnp.exp(-y))
        g = g_ref[:, _chunk(j)].astype(jnp.float32)
        s_ref[:, _chunk(j)] = (g * sig * (1.0 + y * (1.0 - sig))).astype(s_ref.dtype)
        sp_ref[:, _chunk(j)] = jnp.zeros((g_ref.shape[0], CH), jnp.float32)
        return carry

    lax.fori_loop(0, width // CH, pre, 0)

    def body(k):
        r = idx_ref[3 * k]
        c = idx_ref[3 * k + 1]
        back = lax.dot_general(
            s_ref[:, _blk(c)],
            w_vmem[k],
            (((1,), (1,)), ((), ())),
            preferred_element_type=jnp.float32,
        )
        sp_ref[:, _blk(r)] += back * _flag(idx_ref, k)

    _slot_chunks(idx_ref, copies, body)

    def epi(j, carry):
        g = g_ref[:, _chunk(j)].astype(jnp.float32)
        gout_ref[:, _chunk(j)] = (g + sp_ref[:, _chunk(j)]).astype(gout_ref.dtype)
        return carry

    lax.fori_loop(0, width // CH, epi, 0)


def layer_backward(g, y, weights, layer, il):
    rows, width = g.shape
    return pl.pallas_call(
        functools.partial(_bwd_kernel, layer * KMAX),
        out_shape=(
            jax.ShapeDtypeStruct((rows, width), jnp.bfloat16),
            jax.ShapeDtypeStruct((rows, width), jnp.bfloat16),
        ),
        in_specs=[_SMEM, _VMEM, _VMEM, _ANY],
        out_specs=(_VMEM, _VMEM),
        scratch_shapes=[
            pltpu.VMEM((rows, width), jnp.float32),
            pltpu.VMEM((KMAX, BLK, BLK), weights.dtype),
            pltpu.SemaphoreType.DMA((KMAX // NSUB,)),
        ],
        compiler_params=pltpu.CompilerParams(vmem_limit_bytes=VMEM_LIMIT),
    )(il.reshape(-1), g, y, weights)


def _dw_kernel(idx_ref, h_ref, s_ref, dw_ref):
    for j in range(dw_ref.shape[0] // NSUB):

        @pl.when(idx_ref[3 * j * NSUB + 2] > 0)
        def _():
            for k in range(j * NSUB, (j + 1) * NSUB):
                r = idx_ref[3 * k]
                c = idx_ref[3 * k + 1]
                dw_ref[k] = lax.dot_general(
                    h_ref[:, _blk(r)],
                    s_ref[:, _blk(c)],
                    (((0,), (0,)), ((), ())),
                    preferred_element_type=jnp.float32,
                ) * _flag(idx_ref, k)

        @pl.when(idx_ref[3 * j * NSUB + 2] <= 0)
        def _():
            dw_ref[pl.ds(j * NSUB, NSUB)] = jnp.zeros((NSUB, BLK, BLK), jnp.float32)


def layer_dw(h_all, s_all, il):
    return pl.pallas_call(
        _dw_kernel,
        out_shape=jax.ShapeDtypeStruct((il.shape[0], BLK, BLK), jnp.float32),
        in_specs=[_SMEM, _VMEM, _VMEM],
        out_specs=_VMEM,
        compiler_params=pltpu.CompilerParams(vmem_limit_bytes=VMEM_LIMIT),
    )(il.reshape(-1), h_all, s_all)


def on_device(x_in, cotangent, weights, block_index):
    segments = lax.axis_size("segment")
    me_segment = lax.axis_index("segment")
    mbs, rows_dev, width = x_in.shape
    idx = block_index.reshape(LSLOT, KMAX, 3)
    ticks = mbs + segments - 1

    def segment_forward(start):
        h = start
        inputs = []
        preacts = []
        for layer in range(LSLOT):
            h_next, y = layer_forward(h, weights, layer, idx[layer])
            inputs.append(h)
            preacts.append(y)
            h = h_next
        return (h, jnp.stack(inputs), jnp.stack(preacts))

    def skip_forward(start):
        return (
            start,
            jnp.zeros((LSLOT, rows_dev, width), jnp.bfloat16),
            jnp.zeros((LSLOT, rows_dev, width), jnp.float32),
        )

    stash_h = jnp.zeros((mbs + 1, LSLOT, rows_dev, width), jnp.bfloat16)
    stash_y = jnp.zeros((mbs + 1, LSLOT, rows_dev, width), jnp.float32)

    def forward_tick(tick, carry):
        received, saved_h, saved_y = carry
        micro = tick - me_segment
        live = (micro >= 0) & (micro < mbs)
        place_at = jnp.clip(micro, 0, mbs - 1)
        first = lax.dynamic_index_in_dim(x_in, place_at, 0, keepdims=False)
        start = jnp.where(me_segment == 0, first, received)
        h_out, inputs, preacts = lax.cond(live, segment_forward, skip_forward, start)
        store_at = jnp.where(live, place_at, mbs)
        saved_h = lax.dynamic_update_index_in_dim(saved_h, inputs, store_at, 0)
        saved_y = lax.dynamic_update_index_in_dim(saved_y, preacts, store_at, 0)
        received = shifted(h_out, "segment", 1)
        return (received, saved_h, saved_y)

    blank = jnp.zeros((rows_dev, width), jnp.bfloat16)
    unused_recv, stash_h, stash_y = lax.fori_loop(
        0, ticks, forward_tick, (blank, stash_h, stash_y)
    )
    stash_s = jnp.zeros((mbs + 1, LSLOT, rows_dev, width), jnp.bfloat16)

    def backward_tick(tick, carry):
        received, saved_s = carry
        micro = tick - (segments - 1 - me_segment)
        live = (micro >= 0) & (micro < mbs)
        place_at = jnp.clip(micro, 0, mbs - 1)
        top = lax.dynamic_index_in_dim(cotangent, place_at, 0, keepdims=False)
        grad_in = jnp.where(me_segment == segments - 1, top, received)
        layer_y = lax.dynamic_index_in_dim(stash_y, place_at, 0, keepdims=False)

        def run_back(grad):
            s_parts = [None] * LSLOT
            for layer in reversed(range(LSLOT)):
                grad, s_parts[layer] = layer_backward(grad, layer_y[layer], weights, layer, idx[layer])
            return (grad, jnp.stack(s_parts))

        def skip_back(grad):
            return (grad, jnp.zeros((LSLOT, rows_dev, width), jnp.bfloat16))

        grad_out, s_all = lax.cond(live, run_back, skip_back, grad_in)
        saved_s = lax.dynamic_update_index_in_dim(saved_s, s_all, jnp.where(live, place_at, mbs), 0)
        received = shifted(grad_out, "segment", -1)
        return (received, saved_s)

    unused_grad, stash_s = lax.fori_loop(0, ticks, backward_tick, (blank, stash_s))
    dws = []
    for layer in range(LSLOT):
        h_all = stash_h[:mbs, layer].reshape(mbs * rows_dev, width)
        s_all = stash_s[:mbs, layer].reshape(mbs * rows_dev, width)
        dws.append(layer_dw(h_all, s_all, idx[layer]))
    acc = jnp.concatenate(dws, axis=0).astype(jnp.bfloat16)
    return lax.psum_scatter(acc, "dp", scatter_dimension=0, tiled=True).astype(jnp.float32)


def solution(mesh):
    return jax.shard_map(
        on_device,
        mesh=mesh,
        in_specs=(
            P(None, "dp", None),
            P(None, "dp", None),
            P("segment", None, None),
            P("segment", None),
        ),
        out_specs=P(("segment", "dp"), None, None),
        check_vma=False,
    )
```

profile of v0, /device:TPU:0, one launch (start us, length us, event | category | flops | bytes accessed | tf_op | source)
XLA Modules:
  0.0 610.2 jit_solution(10624498800812405370)
XLA Ops:
  8.7 6.0 broadcast_in_dim.46
  19.1 213.9 %while.35 = (s32[]{:T(128)}, bf16[64,8192]{1,0:T(8,128)(2,1)}, bf16[3,2,64,8192]{3,2,1,0:T(8,128)(2,1)}, f32[3,2,64,8192]{3,2,1,0:T(8,128)}, s32[]{:T(128)}, /*i...) while((s32[]{:T(128)}, bf16[64,8192]{1,0:T(8,128)(2,1)}, ...), condition=%wide.region_3.4_spmd, body=%wide.region_0.3_spmd.sunk | while | flops 2621450 | bytes 45101404 | solution.py:228
  20.4 19.2 %conditional.4 = (bf16[64,8192]{1,0:T(8,128)(2,1)}, bf16[1,2,64,8192]{3,2,1,0:T(8,128)(2,1)S(1)}, f32[1,2,64,8192]{3,2,1,0:T(8,128)}) conditional(s32[]{:T(128)} %convert_element_type.24, bf16[64,8192]{1,0:T(8,128)(2,1)S(1)} %bitcast_select_fusion.4, (s32[2,128,3]{2,1,0:T(8,128)S(1)}, bf16[64,8192]{1,0:T(8,128)(2,1)S(1)}, ...), branch_computations={%region_1.1_spmd, %region_2.2_spmd} | conditional | flops 2097152 | bytes 25178192 | solution.py:220
  21.2 6.6 %branch_1_fun.6 = (bf16[64,8192]{1,0:T(8,128)(2,1)}, f32[64,8192]{1,0:T(8,128)}) custom-call(s32[384]{0:T(512)} %squeeze.37.idx_ref, bf16[64,8192]{1,0:T(8,128)(2,1)S(1)} %get-tuple-element.389.h_ref, bf16[256,128,128]{2,1,0:T(8,128)(2,1)} %get-tuple-element.390.w_hbm), custom_call_target="tpu_custom_call" | custom-call | tf_op jit(solution)/shard_map/while/body/eval_jaxpr/cond/branch_1_fun/pallas_call | solution.py:85
  28.7 6.7 %branch_1_fun.7 = (bf16[64,8192]{1,0:T(8,128)(2,1)}, f32[64,8192]{1,0:T(8,128)}) custom-call(s32[384]{0:T(512)} %squeeze.36.idx_ref, bf16[64,8192]{1,0:T(8,128)(2,1)} %get-tuple-element.391.h_ref, bf16[256,128,128]{2,1,0:T(8,128)(2,1)} %get-tuple-element.390.w_hbm), custom_call_target="tpu_custom_call" | custom-call | tf_op jit(solution)/shard_map/while/body/eval_jaxpr/cond/branch_1_fun/pallas_call | solution.py:85
  35.4 4.0 maximum_bitcast_fusion
  43.3 4.5 constant_dynamic-update-slice_fusion.7
  47.9 16.7 %collective-permute-done = bf16[64,8192]{1,0:T(8,128)(2,1)} collective-permute-done((bf16[64,8192]{1,0:T(8,128)(2,1)}, bf16[64,8192]{1,0:T(8,128)(2,1)}, u32[]{:S(2)}, u32[]{:S(2)}) %collective-permute-start) | collective-permute-done | bytes 1048608 | tf_op jit(solution)/shard_map/while/body/eval_jaxpr/ppermute | solution.py:25
  65.9 19.2 %conditional.4 = (bf16[64,8192]{1,0:T(8,128)(2,1)}, bf16[1,2,64,8192]{3,2,1,0:T(8,128)(2,1)S(1)}, f32[1,2,64,8192]{3,2,1,0:T(8,128)}) conditional(s32[]{:T(128)} %convert_element_type.24, bf16[64,8192]{1,0:T(8,128)(2,1)S(1)} %bitcast_select_fusion.4, (s32[2,128,3]{2,1,0:T(8,128)S(1)}, bf16[64,8192]{1,0:T(8,128)(2,1)S(1)}, ...), branch_computations={%region_1.1_spmd, %region_2.2_spmd} | conditional | flops 2097152 | bytes 25178192 | solution.py:220
  66.7 6.6 %branch_1_fun.6 = (bf16[64,8192]{1,0:T(8,128)(2,1)}, f32[64,8192]{1,0:T(8,128)}) custom-call(s32[384]{0:T(512)} %squeeze.37.idx_ref, bf16[64,8192]{1,0:T(8,128)(2,1)S(1)} %get-tuple-element.389.h_ref, bf16[256,128,128]{2,1,0:T(8,128)(2,1)} %get-tuple-element.390.w_hbm), custom_call_target="tpu_custom_call" | custom-call | tf_op jit(solution)/shard_map/while/body/eval_jaxpr/cond/branch_1_fun/pallas_call | solution.py:85
  74.1 6.7 %branch_1_fun.7 = (bf16[64,8192]{1,0:T(8,128)(2,1)}, f32[64,8192]{1,0:T(8,128)}) custom-call(s32[384]{0:T(512)} %squeeze.36.idx_ref, bf16[64,8192]{1,0:T(8,128)(2,1)} %get-tuple-element.391.h_ref, bf16[256,128,128]{2,1,0:T(8,128)(2,1)} %get-tuple-element.390.w_hbm), custom_call_target="tpu_custom_call" | custom-call | tf_op jit(solution)/shard_map/while/body/eval_jaxpr/cond/branch_1_fun/pallas_call | solution.py:85
  80.9 4.0 maximum_bitcast_fusion
  85.1 4.8 collective-permute-start
  91.3 4.6 constant_dynamic-update-slice_fusion.7
  95.9 15.7 %collective-permute-done = bf16[64,8192]{1,0:T(8,128)(2,1)} collective-permute-done((bf16[64,8192]{1,0:T(8,128)(2,1)}, bf16[64,8192]{1,0:T(8,128)(2,1)}, u32[]{:S(2)}, u32[]{:S(2)}) %collective-permute-start) | collective-permute-done | bytes 1048608 | tf_op jit(solution)/shard_map/while/body/eval_jaxpr/ppermute | solution.py:25
  113.0 3.7 conditional.4
  116.7 20.3 %collective-permute-start = (bf16[64,8192]{1,0:T(8,128)(2,1)}, bf16[64,8192]{1,0:T(8,128)(2,1)}, u32[]{:S(2)}, u32[]{:S(2)}) collective-permute-start(bf16[64,8192]{1,0:T(8,128)(2,1)} %get-tuple-element.589), channel_id=1, source_target_pairs={{0,8},{8,16},{16,24},{1,9},{9,17},{17,25},{2,10},{10,18},{18,26},{... | collective-permute-start | bytes 3145736 | tf_op jit(solution)/shard_map/while/body/eval_jaxpr/ppermute | solution.py:25
  138.5 4.6 constant_dynamic-update-slice_fusion.7
  143.0 14.9 %collective-permute-done = bf16[64,8192]{1,0:T(8,128)(2,1)} collective-permute-done((bf16[64,8192]{1,0:T(8,128)(2,1)}, bf16[64,8192]{1,0:T(8,128)(2,1)}, u32[]{:S(2)}, u32[]{:S(2)}) %collective-permute-start) | collective-permute-done | bytes 1048608 | tf_op jit(solution)/shard_map/while/body/eval_jaxpr/ppermute | solution.py:25
  159.3 3.7 conditional.4
  163.0 5.7 collective-permute-start
  170.1 4.6 constant_dynamic-update-slice_fusion.7
  174.7 14.0 %collective-permute-done = bf16[64,8192]{1,0:T(8,128)(2,1)} collective-permute-done((bf16[64,8192]{1,0:T(8,128)(2,1)}, bf16[64,8192]{1,0:T(8,128)(2,1)}, u32[]{:S(2)}, u32[]{:S(2)}) %collective-permute-start) | collective-permute-done | bytes 1048608 | tf_op jit(solution)/shard_map/while/body/eval_jaxpr/ppermute | solution.py:25
  190.0 3.7 conditional.4
  193.7 20.0 %collective-permute-start = (bf16[64,8192]{1,0:T(8,128)(2,1)}, bf16[64,8192]{1,0:T(8,128)(2,1)}, u32[]{:S(2)}, u32[]{:S(2)}) collective-permute-start(bf16[64,8192]{1,0:T(8,128)(2,1)} %get-tuple-element.589), channel_id=1, source_target_pairs={{0,8},{8,16},{16,24},{1,9},{9,17},{17,25},{2,10},{10,18},{18,26},{... | collective-permute-start | bytes 3145736 | tf_op jit(solution)/shard_map/while/body/eval_jaxpr/ppermute | solution.py:25
  215.1 4.6 constant_dynamic-update-slice_fusion.7
  219.6 13.4 %collective-permute-done = bf16[64,8192]{1,0:T(8,128)(2,1)} collective-permute-done((bf16[64,8192]{1,0:T(8,128)(2,1)}, bf16[64,8192]{1,0:T(8,128)(2,1)}, u32[]{:S(2)}, u32[]{:S(2)}) %collective-permute-start) | collective-permute-done | bytes 1048608 | tf_op jit(solution)/shard_map/while/body/eval_jaxpr/ppermute | solution.py:25
  237.5 248.2 %while.36 = (s32[]{:T(128)}, bf16[64,8192]{1,0:T(8,128)(2,1)}, bf16[3,2,64,8192]{3,2,1,0:T(8,128)(2,1)}, s32[]{:T(128)}, pred[]{:T(512)}, /*index=5*/bf16[2,64,8...) while((s32[]{:T(128)}, bf16[64,8192]{1,0:T(8,128)(2,1)}, ...), condition=%wide.region_7.8_spmd, body=%wide.region_4.7_spmd.sunk | while | flops 1572875 | bytes 24129852 | solution.py:256
  242.2 21.6 %collective-permute-done.1 = bf16[64,8192]{1,0:T(8,128)(2,1)} collective-permute-done((bf16[64,8192]{1,0:T(8,128)(2,1)S(1)}, bf16[64,8192]{1,0:T(8,128)(2,1)}, u32[]{:S(2)}, u32[]{:S(2)}) %collective-permute-start.1) | collective-permute-done | bytes 1048608 | tf_op jit(solution)/shard_map/while/body/eval_jaxpr/ppermute | solution.py:25
  268.5 34.1 %collective-permute-done.1 = bf16[64,8192]{1,0:T(8,128)(2,1)} collective-permute-done((bf16[64,8192]{1,0:T(8,128)(2,1)S(1)}, bf16[64,8192]{1,0:T(8,128)(2,1)}, u32[]{:S(2)}, u32[]{:S(2)}) %collective-permute-start.1) | collective-permute-done | bytes 1048608 | tf_op jit(solution)/shard_map/while/body/eval_jaxpr/ppermute | solution.py:25
  307.3 85.2 %collective-permute-done.1 = bf16[64,8192]{1,0:T(8,128)(2,1)} collective-permute-done((bf16[64,8192]{1,0:T(8,128)(2,1)S(1)}, bf16[64,8192]{1,0:T(8,128)(2,1)}, u32[]{:S(2)}, u32[]{:S(2)}) %collective-permute-start.1) | collective-permute-done | bytes 1048608 | tf_op jit(solution)/shard_map/while/body/eval_jaxpr/ppermute | solution.py:25
  394.1 23.5 %conditional.5 = (bf16[64,8192]{1,0:T(8,128)(2,1)S(1)}, bf16[1,2,64,8192]{3,2,1,0:T(8,128)(2,1)S(1)}) conditional(s32[]{:T(128)} %convert_element_type.25, bf16[64,8192]{1,0:T(8,128)(2,1)S(1)} %bitcast_select_fusion.5, (s32[2,128,3]{2,1,0:T(8,128)S(1)}, f32[3,2,64,8192]{3,2,1,0:T(8,128)}, s32[]{:T(128)}, bf16[64,8192]{1,0:T(8,128)(2,1)S(1)}, ...), branch_computations={%region_5.5_spmd, %region_6.6_spmd} | conditional | flops 1048577 | bytes 12595236 | solution.py:251
  394.1 4.7 dynamic-slice_bitcast_fusion
  399.7 7.2 %branch_1_fun.8 = (bf16[64,8192]{1,0:T(8,128)(2,1)}, bf16[64,8192]{1,0:T(8,128)(2,1)}) custom-call(s32[384]{0:T(512)} %squeeze.40.idx_ref, bf16[64,8192]{1,0:T(8,128)(2,1)S(1)} %get-tuple-element.409.g_ref, f32[64,8192]{1,0:T(8,128)} %get-tuple-element.474.y_ref, bf16[256,128,128]{2,1,0:T(8,128)(2,1)} %get-tuple-element.412.w_hbm), custom_call_target="tpu_custom_call" | custom-call | tf_op jit(solution)/shard_map/while/body/eval_jaxpr/cond/branch_1_fun/pallas_call | solution.py:138
  407.7 8.2 %branch_1_fun.9 = (bf16[64,8192]{1,0:T(8,128)(2,1)S(1)}, bf16[64,8192]{1,0:T(8,128)(2,1)}) custom-call(s32[384]{0:T(512)} %squeeze.39.idx_ref, bf16[64,8192]{1,0:T(8,128)(2,1)} %get-tuple-element.413.g_ref, f32[64,8192]{1,0:T(8,128)} %get-tuple-element.473.y_ref, bf16[256,128,128]{2,1,0:T(8,128)(2,1)} %get-tuple-element.412.w_hbm), custom_call_target="tpu_custom_call" | custom-call | tf_op jit(solution)/shard_map/while/body/eval_jaxpr/cond/branch_1_fun/pallas_call | solution.py:138
  420.3 19.2 %collective-permute-done.1 = bf16[64,8192]{1,0:T(8,128)(2,1)} collective-permute-done((bf16[64,8192]{1,0:T(8,128)(2,1)S(1)}, bf16[64,8192]{1,0:T(8,128)(2,1)}, u32[]{:S(2)}, u32[]{:S(2)}) %collective-permute-start.1) | collective-permute-done | bytes 1048608 | tf_op jit(solution)/shard_map/while/body/eval_jaxpr/ppermute | solution.py:25
  441.2 23.4 %conditional.5 = (bf16[64,8192]{1,0:T(8,128)(2,1)S(1)}, bf16[1,2,64,8192]{3,2,1,0:T(8,128)(2,1)S(1)}) conditional(s32[]{:T(128)} %convert_element_type.25, bf16[64,8192]{1,0:T(8,128)(2,1)S(1)} %bitcast_select_fusion.5, (s32[2,128,3]{2,1,0:T(8,128)S(1)}, f32[3,2,64,8192]{3,2,1,0:T(8,128)}, s32[]{:T(128)}, bf16[64,8192]{1,0:T(8,128)(2,1)S(1)}, ...), branch_computations={%region_5.5_spmd, %region_6.6_spmd} | conditional | flops 1048577 | bytes 12595236 | solution.py:251
  441.2 4.7 dynamic-slice_bitcast_fusion
  446.7 7.2 %branch_1_fun.8 = (bf16[64,8192]{1,0:T(8,128)(2,1)}, bf16[64,8192]{1,0:T(8,128)(2,1)}) custom-call(s32[384]{0:T(512)} %squeeze.40.idx_ref, bf16[64,8192]{1,0:T(8,128)(2,1)S(1)} %get-tuple-element.409.g_ref, f32[64,8192]{1,0:T(8,128)} %get-tuple-element.474.y_ref, bf16[256,128,128]{2,1,0:T(8,128)(2,1)} %get-tuple-element.412.w_hbm), custom_call_target="tpu_custom_call" | custom-call | tf_op jit(solution)/shard_map/while/body/eval_jaxpr/cond/branch_1_fun/pallas_call | solution.py:138
  454.7 8.2 %branch_1_fun.9 = (bf16[64,8192]{1,0:T(8,128)(2,1)S(1)}, bf16[64,8192]{1,0:T(8,128)(2,1)}) custom-call(s32[384]{0:T(512)} %squeeze.39.idx_ref, bf16[64,8192]{1,0:T(8,128)(2,1)} %get-tuple-element.413.g_ref, f32[64,8192]{1,0:T(8,128)} %get-tuple-element.473.y_ref, bf16[256,128,128]{2,1,0:T(8,128)(2,1)} %get-tuple-element.412.w_hbm), custom_call_target="tpu_custom_call" | custom-call | tf_op jit(solution)/shard_map/while/body/eval_jaxpr/cond/branch_1_fun/pallas_call | solution.py:138
  467.4 18.3 %collective-permute-done.1 = bf16[64,8192]{1,0:T(8,128)(2,1)} collective-permute-done((bf16[64,8192]{1,0:T(8,128)(2,1)S(1)}, bf16[64,8192]{1,0:T(8,128)(2,1)}, u32[]{:S(2)}, u32[]{:S(2)}) %collective-permute-start.1) | collective-permute-done | bytes 1048608 | tf_op jit(solution)/shard_map/while/body/eval_jaxpr/ppermute | solution.py:25
  485.7 5.0 fusion.2
  494.1 9.6 %shard_map.46 = f32[128,128,128]{2,1,0:T(8,128)} custom-call(s32[384]{0:T(512)} %reshape_squeeze.18.idx_ref, bf16[128,8192]{1,0:T(8,128)(2,1)} %bitcast.39, bf16[128,8192]{1,0:T(8,128)(2,1)} %bitcast.38), custom_call_target="tpu_custom_call" | custom-call | tf_op jit(solution)/shard_map/pallas_call | solution.py:176
  503.6 6.3 %convert.6 = bf16[128,128,128]{2,1,0:T(8,128)(2,1)} convert(f32[128,128,128]{2,1,0:T(8,128)} %shard_map.46) | non-fusion elementwise | flops 2097152 | bytes 12582912 | tf_op jit(solution)/shard_map/convert
  510.9 8.5 %shard_map.47 = f32[128,128,128]{2,1,0:T(8,128)} custom-call(s32[384]{0:T(512)} %reshape_squeeze.21.idx_ref, bf16[128,8192]{1,0:T(8,128)(2,1)} %bitcast.37, bf16[128,8192]{1,0:T(8,128)(2,1)} %bitcast.36), custom_call_target="tpu_custom_call" | custom-call | tf_op jit(solution)/shard_map/pallas_call | solution.py:176
  519.4 6.3 %convert.7 = bf16[128,128,128]{2,1,0:T(8,128)(2,1)} convert(f32[128,128,128]{2,1,0:T(8,128)} %shard_map.47) | non-fusion elementwise | flops 2097152 | bytes 12582912 | tf_op jit(solution)/shard_map/convert.1
  525.8 7.4 %pad_maximum_fusion = bf16[256,128,128]{2,1,0:T(8,128)(2,1)} fusion(bf16[128,128,128]{2,1,0:T(8,128)(2,1)} %convert.7, bf16[128,128,128]{2,1,0:T(8,128)(2,1)} %convert.6), kind=kLoop, calls=%fused_computation.10 | loop fusion | flops 4194304 | bytes 16777216 | tf_op jit(solution)/shard_map/concatenate | solution.py:262
  533.2 67.3 %reduce-scatter.2.cloned.1.call-done = bf16[32,128,128]{2,1,0:T(8,128)(2,1)} async-done(((bf16[256,128,128]{2,1,0:T(8,128)(2,1)}), bf16[32,128,128]{2,1,0:T(8,128)(2,1)}) %reduce-scatter.2.cloned.1.call-update) | async-done | bytes 1048592 | tf_op jit(solution)/shard_map/reduce_scatter | solution.py:263
  (85 shorter events, 78.8 us)
Async XLA Ops:
  6.5 594.0 %reduce-scatter.2.cloned.1.call-start = ((), (), s32[]{:S(2)}) async-start(), calls=%async_computation.1 | async-start | bytes 9437184 | tf_op jit(solution)/shard_map/reduce_scatter | solution.py:263
  28.7 6.7 %copy-start.1 = (f32[64,8192]{1,0:T(8,128)S(1)}, f32[64,8192]{1,0:T(8,128)}, u32[]{:S(2)}) copy-start(f32[64,8192]{1,0:T(8,128)} %get-tuple-element.393) | copy-start | bytes 6291460 | tf_op jit(solution)/shard_map/while/body/eval_jaxpr/cond
  35.4 4.0 copy-start
  39.6 24.9 %collective-permute-start = (bf16[64,8192]{1,0:T(8,128)(2,1)}, bf16[64,8192]{1,0:T(8,128)(2,1)}, u32[]{:S(2)}, u32[]{:S(2)}) collective-permute-start(bf16[64,8192]{1,0:T(8,128)(2,1)} %get-tuple-element.589), channel_id=1, source_target_pairs={{0,8},{8,16},{16,24},{1,9},{9,17},{17,25},{2,10},{10,18},{18,26},{... | collective-permute-start | bytes 3145736 | tf_op jit(solution)/shard_map/while/body/eval_jaxpr/ppermute | solution.py:25
  74.1 6.7 %copy-start.1 = (f32[64,8192]{1,0:T(8,128)S(1)}, f32[64,8192]{1,0:T(8,128)}, u32[]{:S(2)}) copy-start(f32[64,8192]{1,0:T(8,128)} %get-tuple-element.393) | copy-start | bytes 6291460 | tf_op jit(solution)/shard_map/while/body/eval_jaxpr/cond
  80.9 4.0 copy-start
  85.1 26.6 %collective-permute-start = (bf16[64,8192]{1,0:T(8,128)(2,1)}, bf16[64,8192]{1,0:T(8,128)(2,1)}, u32[]{:S(2)}, u32[]{:S(2)}) collective-permute-start(bf16[64,8192]{1,0:T(8,128)(2,1)} %get-tuple-element.589), channel_id=1, source_target_pairs={{0,8},{8,16},{16,24},{1,9},{9,17},{17,25},{2,10},{10,18},{18,26},{... | collective-permute-start | bytes 3145736 | tf_op jit(solution)/shard_map/while/body/eval_jaxpr/ppermute | solution.py:25
  116.7 41.2 %collective-permute-start = (bf16[64,8192]{1,0:T(8,128)(2,1)}, bf16[64,8192]{1,0:T(8,128)(2,1)}, u32[]{:S(2)}, u32[]{:S(2)}) collective-permute-start(bf16[64,8192]{1,0:T(8,128)(2,1)} %get-tuple-element.589), channel_id=1, source_target_pairs={{0,8},{8,16},{16,24},{1,9},{9,17},{17,25},{2,10},{10,18},{18,26},{... | collective-permute-start | bytes 3145736 | tf_op jit(solution)/shard_map/while/body/eval_jaxpr/ppermute | solution.py:25
  163.0 25.7 %collective-permute-start = (bf16[64,8192]{1,0:T(8,128)(2,1)}, bf16[64,8192]{1,0:T(8,128)(2,1)}, u32[]{:S(2)}, u32[]{:S(2)}) collective-permute-start(bf16[64,8192]{1,0:T(8,128)(2,1)} %get-tuple-element.589), channel_id=1, source_target_pairs={{0,8},{8,16},{16,24},{1,9},{9,17},{17,25},{2,10},{10,18},{18,26},{... | collective-permute-start | bytes 3145736 | tf_op jit(solution)/shard_map/while/body/eval_jaxpr/ppermute | solution.py:25
  193.7 39.4 %collective-permute-start = (bf16[64,8192]{1,0:T(8,128)(2,1)}, bf16[64,8192]{1,0:T(8,128)(2,1)}, u32[]{:S(2)}, u32[]{:S(2)}) collective-permute-start(bf16[64,8192]{1,0:T(8,128)(2,1)} %get-tuple-element.589), channel_id=1, source_target_pairs={{0,8},{8,16},{16,24},{1,9},{9,17},{17,25},{2,10},{10,18},{18,26},{... | collective-permute-start | bytes 3145736 | tf_op jit(solution)/shard_map/while/body/eval_jaxpr/ppermute | solution.py:25
  239.4 24.4 %collective-permute-start.1 = (bf16[64,8192]{1,0:T(8,128)(2,1)S(1)}, bf16[64,8192]{1,0:T(8,128)(2,1)}, u32[]{:S(2)}, u32[]{:S(2)}) collective-permute-start(bf16[64,8192]{1,0:T(8,128)(2,1)S(1)} %get-tuple-element.601), channel_id=1, source_target_pairs={{8,0},{16,8},{24,16},{9,1},{17,9},{25,17},{10,2},{18,10},{26,18},{... | collective-permute-start | bytes 3145736 | tf_op jit(solution)/shard_map/while/body/eval_jaxpr/ppermute | solution.py:25
  265.6 36.9 %collective-permute-start.1 = (bf16[64,8192]{1,0:T(8,128)(2,1)S(1)}, bf16[64,8192]{1,0:T(8,128)(2,1)}, u32[]{:S(2)}, u32[]{:S(2)}) collective-permute-start(bf16[64,8192]{1,0:T(8,128)(2,1)S(1)} %get-tuple-element.601), channel_id=1, source_target_pairs={{8,0},{16,8},{24,16},{9,1},{17,9},{25,17},{10,2},{18,10},{26,18},{... | collective-permute-start | bytes 3145736 | tf_op jit(solution)/shard_map/while/body/eval_jaxpr/ppermute | solution.py:25
  304.5 88.0 %collective-permute-start.1 = (bf16[64,8192]{1,0:T(8,128)(2,1)S(1)}, bf16[64,8192]{1,0:T(8,128)(2,1)}, u32[]{:S(2)}, u32[]{:S(2)}) collective-permute-start(bf16[64,8192]{1,0:T(8,128)(2,1)S(1)} %get-tuple-element.601), channel_id=1, source_target_pairs={{8,0},{16,8},{24,16},{9,1},{17,9},{25,17},{10,2},{18,10},{26,18},{... | collective-permute-start | bytes 3145736 | tf_op jit(solution)/shard_map/while/body/eval_jaxpr/ppermute | solution.py:25
  417.6 22.0 %collective-permute-start.1 = (bf16[64,8192]{1,0:T(8,128)(2,1)S(1)}, bf16[64,8192]{1,0:T(8,128)(2,1)}, u32[]{:S(2)}, u32[]{:S(2)}) collective-permute-start(bf16[64,8192]{1,0:T(8,128)(2,1)S(1)} %get-tuple-element.601), channel_id=1, source_target_pairs={{8,0},{16,8},{24,16},{9,1},{17,9},{25,17},{10,2},{18,10},{26,18},{... | collective-permute-start | bytes 3145736 | tf_op jit(solution)/shard_map/while/body/eval_jaxpr/ppermute | solution.py:25
  464.7 21.1 %collective-permute-start.1 = (bf16[64,8192]{1,0:T(8,128)(2,1)S(1)}, bf16[64,8192]{1,0:T(8,128)(2,1)}, u32[]{:S(2)}, u32[]{:S(2)}) collective-permute-start(bf16[64,8192]{1,0:T(8,128)(2,1)S(1)} %get-tuple-element.601), channel_id=1, source_target_pairs={{8,0},{16,8},{24,16},{9,1},{17,9},{25,17},{10,2},{18,10},{26,18},{... | collective-permute-start | bytes 3145736 | tf_op jit(solution)/shard_map/while/body/eval_jaxpr/ppermute | solution.py:25
  485.7 5.0 copy-start.2
  490.7 2.5 copy-start.4
  503.6 6.4 %copy-start.3 = (s32[128,3]{0,1:T(4,128)S(1)}, s32[128,3]{0,1:T(4,128)}, u32[]{:S(2)}) copy-start(s32[128,3]{0,1:T(4,128)} %get-tuple-element.482) | copy-start | bytes 4612
Sparse Core Ops, SparseCore 0:
  533.3 67.1 reduce-scatter.1
where the time goes:
time: 610 us
  waiting for transfers between devices  320 us (52%)
  local copies, waits for them, and re-layouts  91.1 us (15%)
  Pallas kernels  75.6 us (12%)
  starting transfers between devices  59.5 us (10%)
  other arithmetic  49.7 us (8%)
  between operations  13.4 us (2%)
    ppermute x10, waiting for transfers between devices, shifted(): lax.ppermute(value, axis, [(source, source + steps) for source in range(l...  253 us
    reduce_scatter x1, waiting for transfers between devices, on_device(): lax.psum_scatter(acc, 'dp', scatter_dimension=0, tiled=True)  67.3 us
    ppermute x10, starting transfers between devices, shifted(): lax.ppermute(value, axis, [(source, source + steps) for source in range(l...  59.5 us
    pallas_call x4, Pallas kernels, layer_backward(): pl.pallas_call(functools.partial(_bwd_kernel, layer * KMAX), out_shape=(j...  30.8 us
    pallas_call x4, Pallas kernels, layer_forward(): pl.pallas_call(functools.partial(_fwd_kernel, layer * KMAX), out_shape=(j...  26.7 us
    dynamic_update_slice x5, local copies, waits for them, and re-layouts, forward_tick(): saved_y = lax.dynamic_update_index_in_dim(saved_y, preacts, store_at, 0)  22.8 us
    pallas_call x2, Pallas kernels, layer_dw(): pl.pallas_call(_dw_kernel, out_shape=jax.ShapeDtypeStruct((il.shape[0], B...  18.1 us
    another operation x2, other arithmetic  12.7 us
  transfers between devices with their start and end apart: 11, of which 11 were waited for; matrix products, arithmetic and copies ran while one was open for 6% of the time, Pallas kernels for 0%

commit v1 on v0

--- a/solution.py
+++ b/solution.py
@@ -152,34 +152,63 @@
     )(il.reshape(-1), g, y, weights)
 
 
-def _dw_kernel(idx_ref, h_ref, s_ref, dw_ref):
+def _dw_kernel(mbs, idx_ref, h_ref, s_ref, dw_ref):
     for j in range(dw_ref.shape[0] // NSUB):
+        layer = j * NSUB // KMAX
 
         @pl.when(idx_ref[3 * j * NSUB + 2] > 0)
         def _():
             for k in range(j * NSUB, (j + 1) * NSUB):
                 r = idx_ref[3 * k]
                 c = idx_ref[3 * k + 1]
-                dw_ref[k] = lax.dot_general(
-                    h_ref[:, _blk(r)],
-                    s_ref[:, _blk(c)],
-                    (((0,), (0,)), ((), ())),
-                    preferred_element_type=jnp.float32,
-                ) * _flag(idx_ref, k)
+                total = None
+                for m in range(mbs):
+                    part = lax.dot_general(
+                        h_ref[m, layer, :, _blk(r)],
+                        s_ref[m, layer, :, _blk(c)],
+                        (((0,), (0,)), ((), ())),
+                        preferred_element_type=jnp.float32,
+                    )
+                    total = part if total is None else total + part
+                dw_ref[k] = total * _flag(idx_ref, k)
 
         @pl.when(idx_ref[3 * j * NSUB + 2] <= 0)
         def _():
             dw_ref[pl.ds(j * NSUB, NSUB)] = jnp.zeros((NSUB, BLK, BLK), jnp.float32)
 
 
-def layer_dw(h_all, s_all, il):
+def segment_dw(stash_h, stash_s, block_index, mbs):
     return pl.pallas_call(
-        _dw_kernel,
-        out_shape=jax.ShapeDtypeStruct((il.shape[0], BLK, BLK), jnp.float32),
+        functools.partial(_dw_kernel, mbs),
+        out_shape=jax.ShapeDtypeStruct((block_index.shape[0], BLK, BLK), jnp.float32),
         in_specs=[_SMEM, _VMEM, _VMEM],
         out_specs=_VMEM,
         compiler_params=pltpu.CompilerParams(vmem_limit_bytes=VMEM_LIMIT),
-    )(il.reshape(-1), h_all, s_all)
+    )(block_index.reshape(-1), stash_h, stash_s)
+
+
+def _exchange(send, pairs):
+    return lax.ppermute(send.astype(jnp.bfloat16), "dp", pairs).astype(jnp.float32)
+
+
+def dp_reduce_scatter(acc):
+    n = lax.axis_size("dp")
+    if n != 8:
+        return lax.psum_scatter(
+            acc.astype(jnp.bfloat16), "dp", scatter_dimension=0, tiled=True
+        ).astype(jnp.float32)
+    d = lax.axis_index("dp")
+    d0, d1, d2 = d % 2, (d // 2) % 2, d // 4
+    pick = lambda a, i, axis: lax.dynamic_index_in_dim(a, i, axis, keepdims=False)
+    x = acc.reshape((2, 2, 2, acc.shape[0] // 8) + acc.shape[1:])
+    x = pick(x, d0, 2) + _exchange(pick(x, 1 - d0, 2), [(i, i ^ 1) for i in range(8)])
+    core0 = d0 == 0
+    keep = jnp.where(core0, pick(x, d1, 1), pick(x, d2, 0))
+    send = jnp.where(core0, pick(x, 1 - d1, 1), pick(x, 1 - d2, 0))
+    x = keep + _exchange(send, [(i, i ^ (2 if i % 2 == 0 else 4)) for i in range(8)])
+    rem = jnp.where(core0, d2, d1)
+    send = pick(x, 1 - rem, 0)
+    return pick(x, rem, 0) + _exchange(send, [(i, i ^ (4 if i % 2 == 0 else 2)) for i in range(8)])
 
 
 def on_device(x_in, cotangent, weights, block_index):
@@ -254,13 +283,8 @@
         return (received, saved_s)
 
     unused_grad, stash_s = lax.fori_loop(0, ticks, backward_tick, (blank, stash_s))
-    dws = []
-    for layer in range(LSLOT):
-        h_all = stash_h[:mbs, layer].reshape(mbs * rows_dev, width)
-        s_all = stash_s[:mbs, layer].reshape(mbs * rows_dev, width)
-        dws.append(layer_dw(h_all, s_all, idx[layer]))
-    acc = jnp.concatenate(dws, axis=0).astype(jnp.bfloat16)
-    return lax.psum_scatter(acc, "dp", scatter_dimension=0, tiled=True).astype(jnp.float32)
+    acc = segment_dw(stash_h, stash_s, block_index, mbs)
+    return dp_reduce_scatter(acc)
 
 
 def solution(mesh):

time: 610 us -> 568 us (0.931)
  waiting for transfers between devices: 320 us -> 304 us
  between operations: 13.4 us -> 0.11 us
  Pallas kernels: 75.6 us -> 66 us
  other arithmetic: 49.7 us -> 41.8 us
    reduce_scatter x1 -> x0, waiting for transfers between devices: 67.3 us -> none  [on_device(): lax.psum_scatter(acc, 'dp', scatter_dimension=0, tiled=True)]
    ppermute x0 -> x3, waiting for transfers between devices: none -> 48.4 us  [_exchange(): lax.ppermute(send.astype(jnp.bfloat16), 'dp', pairs).astype(jnp.float32)]
    add x0 -> x3, other arithmetic: none -> 14.8 us  [the longest x1 5.93 us: dp_reduce_scatter(): pick(x, d0, 2)]
    another operation x2 -> x0, other arithmetic: 12.7 us -> none
    slice x5 -> x0, local copies, waits for them, and re-layouts: 9 us -> none  [the longest x1 5.03 us: on_device(): s_all = stash_s[:mbs, layer].reshape(mbs * rows_dev, width)]
    concatenate x1 -> x0, other arithmetic: 7.44 us -> none  [on_device(): acc = jnp.concatenate(dws, axis=0).astype(jnp.bfloat16)]
    convert_element_type x0 -> x2, local copies, waits for them, and re-layouts: none -> 6.53 us  [_exchange(): send.astype(jnp.bfloat16)]
    pallas_call x2 -> x1, Pallas kernels: 18.1 us -> 15.7 us  [segment_dw(): pl.pallas_call(functools.partial(_dw_kernel, mbs), out_shape=jax.ShapeDty...]
  transfers between devices with their start and end apart: 11 -> 13, of which waited for: 11 -> 13; matrix products, arithmetic and copies ran while one was open for 6% -> 7% of each run, Pallas kernels for 0% -> 0%
where the time goes in v1:
time: 568 us; the launch traced here: 567 us
  waiting for transfers between devices  304 us (54%)
  local copies, waits for them, and re-layouts  92.9 us (16%)
  Pallas kernels  66 us (12%)
  starting transfers between devices  61.5 us (11%)
  other arithmetic  41.8 us (7%)
    ppermute x10, waiting for transfers between devices, shifted(): lax.ppermute(value, axis, [(source, source + steps) for source in range(l...  256 us
    ppermute x10, starting transfers between devices, shifted(): lax.ppermute(value, axis, [(source, source + steps) for source in range(l...  61.4 us
    ppermute x3, waiting for transfers between devices, _exchange(): lax.ppermute(send.astype(jnp.bfloat16), 'dp', pairs).astype(jnp.float32)  48.4 us
    pallas_call x4, Pallas kernels, layer_backward(): pl.pallas_call(functools.partial(_bwd_kernel, layer * KMAX), out_shape=(j...  26 us
    pallas_call x4, Pallas kernels, layer_forward(): pl.pallas_call(functools.partial(_fwd_kernel, layer * KMAX), out_shape=(j...  24.2 us
    dynamic_update_slice x5, local copies, waits for them, and re-layouts, forward_tick(): saved_y = lax.dynamic_update_index_in_dim(saved_y, preacts, store_at, 0)  22.8 us
    pallas_call x1, Pallas kernels, segment_dw(): pl.pallas_call(functools.partial(_dw_kernel, mbs), out_shape=jax.ShapeDty...  15.7 us
  transfers between devices with their start and end apart: 13, of which 13 were waited for; matrix products, arithmetic and copies ran while one was open for 7% of the time, Pallas kernels for 0%

profile of v1, /device:TPU:0, one launch (start us, length us, event | category | flops | bytes accessed | tf_op | source)
XLA Modules:
  0.0 566.9 jit_solution(11157474745942679766)
XLA Ops:
  1.6 6.1 %broadcast_in_dim.46 = f32[3,2,64,8192]{3,2,1,0:T(8,128)} broadcast(f32[]{:T(128)} %constant.177.clone.1), dimensions={} | broadcast | bytes 12582916 | tf_op jit(solution)/shard_map/broadcast_in_dim | solution.py:240
  12.1 212.9 %while.35 = (s32[]{:T(128)}, bf16[64,8192]{1,0:T(8,128)(2,1)}, bf16[3,2,64,8192]{3,2,1,0:T(8,128)(2,1)}, f32[3,2,64,8192]{3,2,1,0:T(8,128)}, s32[]{:T(128)}, /*i...) while((s32[]{:T(128)}, bf16[64,8192]{1,0:T(8,128)(2,1)}, ...), condition=%wide.region_3.4_spmd, body=%wide.region_0.3_spmd.sunk | while | flops 2621450 | bytes 45101404 | solution.py:257
  13.5 17.9 %conditional.4 = (bf16[64,8192]{1,0:T(8,128)(2,1)}, bf16[1,2,64,8192]{3,2,1,0:T(8,128)(2,1)S(1)}, f32[1,2,64,8192]{3,2,1,0:T(8,128)}) conditional(s32[]{:T(128)} %convert_element_type.61, bf16[64,8192]{1,0:T(8,128)(2,1)S(1)} %bitcast_select_fusion.6, (s32[2,128,3]{2,1,0:T(8,128)S(1)}, bf16[64,8192]{1,0:T(8,128)(2,1)S(1)}, ...), branch_computations={%region_1.1_spmd, %region_2.2_spmd} | conditional | flops 2097152 | bytes 25178192 | solution.py:249
  14.3 5.4 branch_1_fun.6
  20.5 6.7 %branch_1_fun.7 = (bf16[64,8192]{1,0:T(8,128)(2,1)}, f32[64,8192]{1,0:T(8,128)}) custom-call(s32[384]{0:T(512)} %squeeze.54.idx_ref, bf16[64,8192]{1,0:T(8,128)(2,1)} %get-tuple-element.391.h_ref, bf16[256,128,128]{2,1,0:T(8,128)(2,1)} %get-tuple-element.390.w_hbm), custom_call_target="tpu_custom_call" | custom-call | tf_op jit(solution)/shard_map/while/body/eval_jaxpr/cond/branch_1_fun/pallas_call | solution.py:85
  27.2 3.9 maximum_bitcast_fusion
  35.1 4.5 constant_dynamic-update-slice_fusion.7
  39.7 16.6 %collective-permute-done = bf16[64,8192]{1,0:T(8,128)(2,1)} collective-permute-done((bf16[64,8192]{1,0:T(8,128)(2,1)}, bf16[64,8192]{1,0:T(8,128)(2,1)}, u32[]{:S(2)}, u32[]{:S(2)}) %collective-permute-start) | collective-permute-done | bytes 1048608 | tf_op jit(solution)/shard_map/while/body/eval_jaxpr/ppermute | solution.py:25
  57.6 17.9 %conditional.4 = (bf16[64,8192]{1,0:T(8,128)(2,1)}, bf16[1,2,64,8192]{3,2,1,0:T(8,128)(2,1)S(1)}, f32[1,2,64,8192]{3,2,1,0:T(8,128)}) conditional(s32[]{:T(128)} %convert_element_type.61, bf16[64,8192]{1,0:T(8,128)(2,1)S(1)} %bitcast_select_fusion.6, (s32[2,128,3]{2,1,0:T(8,128)S(1)}, bf16[64,8192]{1,0:T(8,128)(2,1)S(1)}, ...), branch_computations={%region_1.1_spmd, %region_2.2_spmd} | conditional | flops 2097152 | bytes 25178192 | solution.py:249
  58.5 5.4 branch_1_fun.6
  64.7 6.7 %branch_1_fun.7 = (bf16[64,8192]{1,0:T(8,128)(2,1)}, f32[64,8192]{1,0:T(8,128)}) custom-call(s32[384]{0:T(512)} %squeeze.54.idx_ref, bf16[64,8192]{1,0:T(8,128)(2,1)} %get-tuple-element.391.h_ref, bf16[256,128,128]{2,1,0:T(8,128)(2,1)} %get-tuple-element.390.w_hbm), custom_call_target="tpu_custom_call" | custom-call | tf_op jit(solution)/shard_map/while/body/eval_jaxpr/cond/branch_1_fun/pallas_call | solution.py:85
  71.4 3.9 maximum_bitcast_fusion
  75.5 6.6 %collective-permute-start = (bf16[64,8192]{1,0:T(8,128)(2,1)}, bf16[64,8192]{1,0:T(8,128)(2,1)}, u32[]{:S(2)}, u32[]{:S(2)}) collective-permute-start(bf16[64,8192]{1,0:T(8,128)(2,1)} %get-tuple-element.583), channel_id=1, source_target_pairs={{0,8},{8,16},{16,24},{1,9},{9,17},{17,25},{2,10},{10,18},{18,26},{... | collective-permute-start | bytes 3145736 | tf_op jit(solution)/shard_map/while/body/eval_jaxpr/ppermute | solution.py:25
  83.6 4.6 constant_dynamic-update-slice_fusion.7
  88.2 15.8 %collective-permute-done = bf16[64,8192]{1,0:T(8,128)(2,1)} collective-permute-done((bf16[64,8192]{1,0:T(8,128)(2,1)}, bf16[64,8192]{1,0:T(8,128)(2,1)}, u32[]{:S(2)}, u32[]{:S(2)}) %collective-permute-start) | collective-permute-done | bytes 1048608 | tf_op jit(solution)/shard_map/while/body/eval_jaxpr/ppermute | solution.py:25
  105.3 3.6 conditional.4
  108.9 20.9 %collective-permute-start = (bf16[64,8192]{1,0:T(8,128)(2,1)}, bf16[64,8192]{1,0:T(8,128)(2,1)}, u32[]{:S(2)}, u32[]{:S(2)}) collective-permute-start(bf16[64,8192]{1,0:T(8,128)(2,1)} %get-tuple-element.583), channel_id=1, source_target_pairs={{0,8},{8,16},{16,24},{1,9},{9,17},{17,25},{2,10},{10,18},{18,26},{... | collective-permute-start | bytes 3145736 | tf_op jit(solution)/shard_map/while/body/eval_jaxpr/ppermute | solution.py:25
  131.3 4.6 constant_dynamic-update-slice_fusion.7
  135.8 14.9 %collective-permute-done = bf16[64,8192]{1,0:T(8,128)(2,1)} collective-permute-done((bf16[64,8192]{1,0:T(8,128)(2,1)}, bf16[64,8192]{1,0:T(8,128)(2,1)}, u32[]{:S(2)}, u32[]{:S(2)}) %collective-permute-start) | collective-permute-done | bytes 1048608 | tf_op jit(solution)/shard_map/while/body/eval_jaxpr/ppermute | solution.py:25
  152.0 3.6 conditional.4
  155.6 5.7 %collective-permute-start = (bf16[64,8192]{1,0:T(8,128)(2,1)}, bf16[64,8192]{1,0:T(8,128)(2,1)}, u32[]{:S(2)}, u32[]{:S(2)}) collective-permute-start(bf16[64,8192]{1,0:T(8,128)(2,1)} %get-tuple-element.583), channel_id=1, source_target_pairs={{0,8},{8,16},{16,24},{1,9},{9,17},{17,25},{2,10},{10,18},{18,26},{... | collective-permute-start | bytes 3145736 | tf_op jit(solution)/shard_map/while/body/eval_jaxpr/ppermute | solution.py:25
  162.8 4.6 constant_dynamic-update-slice_fusion.7
  167.4 13.9 %collective-permute-done = bf16[64,8192]{1,0:T(8,128)(2,1)} collective-permute-done((bf16[64,8192]{1,0:T(8,128)(2,1)}, bf16[64,8192]{1,0:T(8,128)(2,1)}, u32[]{:S(2)}, u32[]{:S(2)}) %collective-permute-start) | collective-permute-done | bytes 1048608 | tf_op jit(solution)/shard_map/while/body/eval_jaxpr/ppermute | solution.py:25
  182.6 3.6 conditional.4
  186.2 19.4 %collective-permute-start = (bf16[64,8192]{1,0:T(8,128)(2,1)}, bf16[64,8192]{1,0:T(8,128)(2,1)}, u32[]{:S(2)}, u32[]{:S(2)}) collective-permute-start(bf16[64,8192]{1,0:T(8,128)(2,1)} %get-tuple-element.583), channel_id=1, source_target_pairs={{0,8},{8,16},{16,24},{1,9},{9,17},{17,25},{2,10},{10,18},{18,26},{... | collective-permute-start | bytes 3145736 | tf_op jit(solution)/shard_map/while/body/eval_jaxpr/ppermute | solution.py:25
  207.1 4.6 constant_dynamic-update-slice_fusion.7
  211.7 13.3 %collective-permute-done = bf16[64,8192]{1,0:T(8,128)(2,1)} collective-permute-done((bf16[64,8192]{1,0:T(8,128)(2,1)}, bf16[64,8192]{1,0:T(8,128)(2,1)}, u32[]{:S(2)}, u32[]{:S(2)}) %collective-permute-start) | collective-permute-done | bytes 1048608 | tf_op jit(solution)/shard_map/while/body/eval_jaxpr/ppermute | solution.py:25
  229.5 246.3 %while.36 = (s32[]{:T(128)}, bf16[64,8192]{1,0:T(8,128)(2,1)}, bf16[3,2,64,8192]{3,2,1,0:T(8,128)(2,1)}, s32[]{:T(128)}, pred[]{:T(512)}, /*index=5*/bf16[2,64,8...) while((s32[]{:T(128)}, bf16[64,8192]{1,0:T(8,128)(2,1)}, ...), condition=%wide.region_7.8_spmd, body=%wide.region_4.7_spmd.sunk | while | flops 1572875 | bytes 24129852 | solution.py:285
  234.1 21.6 %collective-permute-done.1 = bf16[64,8192]{1,0:T(8,128)(2,1)} collective-permute-done((bf16[64,8192]{1,0:T(8,128)(2,1)S(1)}, bf16[64,8192]{1,0:T(8,128)(2,1)}, u32[]{:S(2)}, u32[]{:S(2)}) %collective-permute-start.1) | collective-permute-done | bytes 1048608 | tf_op jit(solution)/shard_map/while/body/eval_jaxpr/ppermute | solution.py:25
  260.4 34.5 %collective-permute-done.1 = bf16[64,8192]{1,0:T(8,128)(2,1)} collective-permute-done((bf16[64,8192]{1,0:T(8,128)(2,1)S(1)}, bf16[64,8192]{1,0:T(8,128)(2,1)}, u32[]{:S(2)}, u32[]{:S(2)}) %collective-permute-start.1) | collective-permute-done | bytes 1048608 | tf_op jit(solution)/shard_map/while/body/eval_jaxpr/ppermute | solution.py:25
  299.5 86.3 %collective-permute-done.1 = bf16[64,8192]{1,0:T(8,128)(2,1)} collective-permute-done((bf16[64,8192]{1,0:T(8,128)(2,1)S(1)}, bf16[64,8192]{1,0:T(8,128)(2,1)}, u32[]{:S(2)}, u32[]{:S(2)}) %collective-permute-start.1) | collective-permute-done | bytes 1048608 | tf_op jit(solution)/shard_map/while/body/eval_jaxpr/ppermute | solution.py:25
  387.5 21.0 %conditional.5 = (bf16[64,8192]{1,0:T(8,128)(2,1)S(1)}, bf16[1,2,64,8192]{3,2,1,0:T(8,128)(2,1)S(1)}) conditional(s32[]{:T(128)} %convert_element_type.62, bf16[64,8192]{1,0:T(8,128)(2,1)S(1)} %bitcast_select_fusion.7, (s32[2,128,3]{2,1,0:T(8,128)S(1)}, f32[3,2,64,8192]{3,2,1,0:T(8,128)}, s32[]{:T(128)}, bf16[64,8192]{1,0:T(8,128)(2,1)S(1)}, ...), branch_computations={%region_5.5_spmd, %region_6.6_spmd} | conditional | flops 1048577 | bytes 12595236 | solution.py:280
  387.5 4.7 dynamic-slice_bitcast_fusion
  392.9 7.2 %branch_1_fun.8 = (bf16[64,8192]{1,0:T(8,128)(2,1)}, bf16[64,8192]{1,0:T(8,128)(2,1)}) custom-call(s32[384]{0:T(512)} %squeeze.58.idx_ref, bf16[64,8192]{1,0:T(8,128)(2,1)S(1)} %get-tuple-element.409.g_ref, f32[64,8192]{1,0:T(8,128)} %get-tuple-element.474.y_ref, bf16[256,128,128]{2,1,0:T(8,128)(2,1)} %get-tuple-element.412.w_hbm), custom_call_target="tpu_custom_call" | custom-call | tf_op jit(solution)/shard_map/while/body/eval_jaxpr/cond/branch_1_fun/pallas_call | solution.py:138
  400.9 5.8 %branch_1_fun.9 = (bf16[64,8192]{1,0:T(8,128)(2,1)S(1)}, bf16[64,8192]{1,0:T(8,128)(2,1)}) custom-call(s32[384]{0:T(512)} %squeeze.57.idx_ref, bf16[64,8192]{1,0:T(8,128)(2,1)} %get-tuple-element.413.g_ref, f32[64,8192]{1,0:T(8,128)} %get-tuple-element.473.y_ref, bf16[256,128,128]{2,1,0:T(8,128)(2,1)} %get-tuple-element.412.w_hbm), custom_call_target="tpu_custom_call" | custom-call | tf_op jit(solution)/shard_map/while/body/eval_jaxpr/cond/branch_1_fun/pallas_call | solution.py:138
  411.3 20.7 %collective-permute-done.1 = bf16[64,8192]{1,0:T(8,128)(2,1)} collective-permute-done((bf16[64,8192]{1,0:T(8,128)(2,1)S(1)}, bf16[64,8192]{1,0:T(8,128)(2,1)}, u32[]{:S(2)}, u32[]{:S(2)}) %collective-permute-start.1) | collective-permute-done | bytes 1048608 | tf_op jit(solution)/shard_map/while/body/eval_jaxpr/ppermute | solution.py:25
  433.7 21.0 %conditional.5 = (bf16[64,8192]{1,0:T(8,128)(2,1)S(1)}, bf16[1,2,64,8192]{3,2,1,0:T(8,128)(2,1)S(1)}) conditional(s32[]{:T(128)} %convert_element_type.62, bf16[64,8192]{1,0:T(8,128)(2,1)S(1)} %bitcast_select_fusion.7, (s32[2,128,3]{2,1,0:T(8,128)S(1)}, f32[3,2,64,8192]{3,2,1,0:T(8,128)}, s32[]{:T(128)}, bf16[64,8192]{1,0:T(8,128)(2,1)S(1)}, ...), branch_computations={%region_5.5_spmd, %region_6.6_spmd} | conditional | flops 1048577 | bytes 12595236 | solution.py:280
  433.7 4.7 dynamic-slice_bitcast_fusion
  439.2 7.2 %branch_1_fun.8 = (bf16[64,8192]{1,0:T(8,128)(2,1)}, bf16[64,8192]{1,0:T(8,128)(2,1)}) custom-call(s32[384]{0:T(512)} %squeeze.58.idx_ref, bf16[64,8192]{1,0:T(8,128)(2,1)S(1)} %get-tuple-element.409.g_ref, f32[64,8192]{1,0:T(8,128)} %get-tuple-element.474.y_ref, bf16[256,128,128]{2,1,0:T(8,128)(2,1)} %get-tuple-element.412.w_hbm), custom_call_target="tpu_custom_call" | custom-call | tf_op jit(solution)/shard_map/while/body/eval_jaxpr/cond/branch_1_fun/pallas_call | solution.py:138
  447.2 5.8 %branch_1_fun.9 = (bf16[64,8192]{1,0:T(8,128)(2,1)S(1)}, bf16[64,8192]{1,0:T(8,128)(2,1)}) custom-call(s32[384]{0:T(512)} %squeeze.57.idx_ref, bf16[64,8192]{1,0:T(8,128)(2,1)} %get-tuple-element.413.g_ref, f32[64,8192]{1,0:T(8,128)} %get-tuple-element.473.y_ref, bf16[256,128,128]{2,1,0:T(8,128)(2,1)} %get-tuple-element.412.w_hbm), custom_call_target="tpu_custom_call" | custom-call | tf_op jit(solution)/shard_map/while/body/eval_jaxpr/cond/branch_1_fun/pallas_call | solution.py:138
  457.6 18.2 %collective-permute-done.1 = bf16[64,8192]{1,0:T(8,128)(2,1)} collective-permute-done((bf16[64,8192]{1,0:T(8,128)(2,1)S(1)}, bf16[64,8192]{1,0:T(8,128)(2,1)}, u32[]{:S(2)}, u32[]{:S(2)}) %collective-permute-start.1) | collective-permute-done | bytes 1048608 | tf_op jit(solution)/shard_map/while/body/eval_jaxpr/ppermute | solution.py:25
  475.8 15.7 %shard_map.46 = f32[256,128,128]{2,1,0:T(8,128)} custom-call(s32[768]{0:T(1024)} %reshape.15.idx_ref, bf16[3,2,64,8192]{3,2,1,0:T(8,128)(2,1)} %get-tuple-element.432.h_ref, bf16[3,2,64,8192]{3,2,1,0:T(8,128)(2,1)} %get-tuple-element.434.s_ref), custom_call_target="tpu_custom_call" | custom-call | tf_op jit(solution)/shard_map/pallas_call | solution.py:181
  491.5 6.4 %fusion = bf16[2,2,32,128,128]{4,3,2,1,0:T(8,128)(2,1)} fusion(f32[2,2,2,32,128,128]{5,4,3,2,1,0:T(8,128)} %bitcast.50, s32[]{:T(128)S(6)} %select_n.140), kind=kLoop, calls=%fused_computation.12 | loop fusion | bytes 8388612 | tf_op jit(solution)/shard_map/convert_element_type | solution.py:191
  497.9 7.5 %collective-permute-done.2 = bf16[2,2,32,128,128]{4,3,2,1,0:T(8,128)(2,1)} collective-permute-done((bf16[2,2,32,128,128]{4,3,2,1,0:T(8,128)(2,1)}, bf16[2,2,32,128,128]{4,3,2,1,0:T(8,128)(2,1)}, u32[]{:S(2)}, u32[]{:S(2)}) %collective-permute-start.2) | collective-permute-done | bytes 4194336 | tf_op jit(solution)/shard_map/ppermute | solution.py:191
  505.4 5.9 %bitcast_add_fusion = f32[2,2,32,128,128]{4,3,2,1,0:T(8,128)S(1)} fusion(bf16[2,2,32,128,128]{4,3,2,1,0:T(8,128)(2,1)} %collective-permute-done.2, f32[2,2,2,32,128,128]{5,4,3,2,1,0:T(8,128)} %bitcast.51, s32[]{:T(128)S(6)} %select_n.139), kind=kLoop, calls=%fused_computation.10 | loop fusion | flops 4194304 | bytes 20971524 | tf_op jit(solution)/shard_map/add | solution.py:204
  515.0 26.1 %collective-permute-done.3 = bf16[2,32,128,128]{3,2,1,0:T(8,128)(2,1)} collective-permute-done((bf16[2,32,128,128]{3,2,1,0:T(8,128)(2,1)S(1)}, bf16[2,32,128,128]{3,2,1,0:T(8,128)(2,1)}, u32[]{:S(2)}, u32[]{:S(2)}) %collective-permute-start.3) | collective-permute-done | bytes 2097184 | tf_op jit(solution)/shard_map/ppermute | solution.py:191
  541.1 5.6 fusion.2
  548.9 14.8 %collective-permute-done.4 = bf16[32,128,128]{2,1,0:T(8,128)(2,1)S(1)} collective-permute-done((bf16[32,128,128]{2,1,0:T(8,128)(2,1)S(1)}, bf16[32,128,128]{2,1,0:T(8,128)(2,1)S(1)}, u32[]{:S(2)}, u32[]{:S(2)}) %collective-permute-start.4) | collective-permute-done | bytes 1048608 | tf_op jit(solution)/shard_map/ppermute | solution.py:191
  (81 shorter events, 80.3 us)
Async XLA Ops:
  20.5 6.7 %copy-start.2 = (f32[64,8192]{1,0:T(8,128)S(1)}, f32[64,8192]{1,0:T(8,128)}, u32[]{:S(2)}) copy-start(f32[64,8192]{1,0:T(8,128)} %get-tuple-element.393) | copy-start | bytes 6291460 | tf_op jit(solution)/shard_map/while/body/eval_jaxpr/cond
  27.2 3.9 copy-start
  31.4 24.9 %collective-permute-start = (bf16[64,8192]{1,0:T(8,128)(2,1)}, bf16[64,8192]{1,0:T(8,128)(2,1)}, u32[]{:S(2)}, u32[]{:S(2)}) collective-permute-start(bf16[64,8192]{1,0:T(8,128)(2,1)} %get-tuple-element.583), channel_id=1, source_target_pairs={{0,8},{8,16},{16,24},{1,9},{9,17},{17,25},{2,10},{10,18},{18,26},{... | collective-permute-start | bytes 3145736 | tf_op jit(solution)/shard_map/while/body/eval_jaxpr/ppermute | solution.py:25
  64.7 6.7 %copy-start.2 = (f32[64,8192]{1,0:T(8,128)S(1)}, f32[64,8192]{1,0:T(8,128)}, u32[]{:S(2)}) copy-start(f32[64,8192]{1,0:T(8,128)} %get-tuple-element.393) | copy-start | bytes 6291460 | tf_op jit(solution)/shard_map/while/body/eval_jaxpr/cond
  71.4 3.9 copy-start
  75.5 28.4 %collective-permute-start = (bf16[64,8192]{1,0:T(8,128)(2,1)}, bf16[64,8192]{1,0:T(8,128)(2,1)}, u32[]{:S(2)}, u32[]{:S(2)}) collective-permute-start(bf16[64,8192]{1,0:T(8,128)(2,1)} %get-tuple-element.583), channel_id=1, source_target_pairs={{0,8},{8,16},{16,24},{1,9},{9,17},{17,25},{2,10},{10,18},{18,26},{... | collective-permute-start | bytes 3145736 | tf_op jit(solution)/shard_map/while/body/eval_jaxpr/ppermute | solution.py:25
  108.9 41.8 %collective-permute-start = (bf16[64,8192]{1,0:T(8,128)(2,1)}, bf16[64,8192]{1,0:T(8,128)(2,1)}, u32[]{:S(2)}, u32[]{:S(2)}) collective-permute-start(bf16[64,8192]{1,0:T(8,128)(2,1)} %get-tuple-element.583), channel_id=1, source_target_pairs={{0,8},{8,16},{16,24},{1,9},{9,17},{17,25},{2,10},{10,18},{18,26},{... | collective-permute-start | bytes 3145736 | tf_op jit(solution)/shard_map/while/body/eval_jaxpr/ppermute | solution.py:25
  155.6 25.7 %collective-permute-start = (bf16[64,8192]{1,0:T(8,128)(2,1)}, bf16[64,8192]{1,0:T(8,128)(2,1)}, u32[]{:S(2)}, u32[]{:S(2)}) collective-permute-start(bf16[64,8192]{1,0:T(8,128)(2,1)} %get-tuple-element.583), channel_id=1, source_target_pairs={{0,8},{8,16},{16,24},{1,9},{9,17},{17,25},{2,10},{10,18},{18,26},{... | collective-permute-start | bytes 3145736 | tf_op jit(solution)/shard_map/while/body/eval_jaxpr/ppermute | solution.py:25
  186.2 38.8 %collective-permute-start = (bf16[64,8192]{1,0:T(8,128)(2,1)}, bf16[64,8192]{1,0:T(8,128)(2,1)}, u32[]{:S(2)}, u32[]{:S(2)}) collective-permute-start(bf16[64,8192]{1,0:T(8,128)(2,1)} %get-tuple-element.583), channel_id=1, source_target_pairs={{0,8},{8,16},{16,24},{1,9},{9,17},{17,25},{2,10},{10,18},{18,26},{... | collective-permute-start | bytes 3145736 | tf_op jit(solution)/shard_map/while/body/eval_jaxpr/ppermute | solution.py:25
  231.3 24.4 %collective-permute-start.1 = (bf16[64,8192]{1,0:T(8,128)(2,1)S(1)}, bf16[64,8192]{1,0:T(8,128)(2,1)}, u32[]{:S(2)}, u32[]{:S(2)}) collective-permute-start(bf16[64,8192]{1,0:T(8,128)(2,1)S(1)} %get-tuple-element.595), channel_id=1, source_target_pairs={{8,0},{16,8},{24,16},{9,1},{17,9},{25,17},{10,2},{18,10},{26,18},{... | collective-permute-start | bytes 3145736 | tf_op jit(solution)/shard_map/while/body/eval_jaxpr/ppermute | solution.py:25
  257.6 37.2 %collective-permute-start.1 = (bf16[64,8192]{1,0:T(8,128)(2,1)S(1)}, bf16[64,8192]{1,0:T(8,128)(2,1)}, u32[]{:S(2)}, u32[]{:S(2)}) collective-permute-start(bf16[64,8192]{1,0:T(8,128)(2,1)S(1)} %get-tuple-element.595), channel_id=1, source_target_pairs={{8,0},{16,8},{24,16},{9,1},{17,9},{25,17},{10,2},{18,10},{26,18},{... | collective-permute-start | bytes 3145736 | tf_op jit(solution)/shard_map/while/body/eval_jaxpr/ppermute | solution.py:25
  296.7 89.1 %collective-permute-start.1 = (bf16[64,8192]{1,0:T(8,128)(2,1)S(1)}, bf16[64,8192]{1,0:T(8,128)(2,1)}, u32[]{:S(2)}, u32[]{:S(2)}) collective-permute-start(bf16[64,8192]{1,0:T(8,128)(2,1)S(1)} %get-tuple-element.595), channel_id=1, source_target_pairs={{8,0},{16,8},{24,16},{9,1},{17,9},{25,17},{10,2},{18,10},{26,18},{... | collective-permute-start | bytes 3145736 | tf_op jit(solution)/shard_map/while/body/eval_jaxpr/ppermute | solution.py:25
  408.5 23.5 %collective-permute-start.1 = (bf16[64,8192]{1,0:T(8,128)(2,1)S(1)}, bf16[64,8192]{1,0:T(8,128)(2,1)}, u32[]{:S(2)}, u32[]{:S(2)}) collective-permute-start(bf16[64,8192]{1,0:T(8,128)(2,1)S(1)} %get-tuple-element.595), channel_id=1, source_target_pairs={{8,0},{16,8},{24,16},{9,1},{17,9},{25,17},{10,2},{18,10},{26,18},{... | collective-permute-start | bytes 3145736 | tf_op jit(solution)/shard_map/while/body/eval_jaxpr/ppermute | solution.py:25
  454.8 21.0 %collective-permute-start.1 = (bf16[64,8192]{1,0:T(8,128)(2,1)S(1)}, bf16[64,8192]{1,0:T(8,128)(2,1)}, u32[]{:S(2)}, u32[]{:S(2)}) collective-permute-start(bf16[64,8192]{1,0:T(8,128)(2,1)S(1)} %get-tuple-element.595), channel_id=1, source_target_pairs={{8,0},{16,8},{24,16},{9,1},{17,9},{25,17},{10,2},{18,10},{26,18},{... | collective-permute-start | bytes 3145736 | tf_op jit(solution)/shard_map/while/body/eval_jaxpr/ppermute | solution.py:25
  497.9 7.5 %collective-permute-start.2 = (bf16[2,2,32,128,128]{4,3,2,1,0:T(8,128)(2,1)}, bf16[2,2,32,128,128]{4,3,2,1,0:T(8,128)(2,1)}, u32[]{:S(2)}, u32[]{:S(2)}) collective-permute-start(bf16[2,2,32,128,128]{4,3,2,1,0:T(8,128)(2,1)} %fusion), channel_id=1, source_target_pairs={{0,1},{1,0},{2,3},{3,2},{4,5},{5,4},{6,7},{7,6},{8,9},{9,8},{10,11... | collective-permute-start | bytes 12582920 | tf_op jit(solution)/shard_map/ppermute | solution.py:191
  511.3 3.2 copy-start.1
  514.9 26.2 %collective-permute-start.3 = (bf16[2,32,128,128]{3,2,1,0:T(8,128)(2,1)S(1)}, bf16[2,32,128,128]{3,2,1,0:T(8,128)(2,1)}, u32[]{:S(2)}, u32[]{:S(2)}) collective-permute-start(bf16[2,32,128,128]{3,2,1,0:T(8,128)(2,1)S(1)} %fusion.1), channel_id=1, source_target_pairs={{0,2},{1,5},{2,0},{3,7},{4,6},{5,1},{6,4},{7,3},{8,10},{9,13},{10,... | collective-permute-start | bytes 6291464 | tf_op jit(solution)/shard_map/ppermute | solution.py:191
  546.7 1.9 copy-start.3
  548.8 14.9 %collective-permute-start.4 = (bf16[32,128,128]{2,1,0:T(8,128)(2,1)S(1)}, bf16[32,128,128]{2,1,0:T(8,128)(2,1)S(1)}, u32[]{:S(2)}, u32[]{:S(2)}) collective-permute-start(bf16[32,128,128]{2,1,0:T(8,128)(2,1)S(1)} %fusion.3), channel_id=1, source_target_pairs={{0,4},{1,3},{2,6},{3,1},{4,0},{5,7},{6,2},{7,5},{8,12},{9,11},{10,... | collective-permute-start | bytes 3145736 | tf_op jit(solution)/shard_map/ppermute | solution.py:191

commit v2 on v1

--- a/solution.py
+++ b/solution.py
@@ -48,82 +48,101 @@
     return copies
 
 
-def _slot_chunks(idx_ref, copies, body):
+def _slot_chunks(idx_ref, base, copies, body):
     for j, copy in enumerate(copies):
         copy.wait()
 
-        @pl.when(idx_ref[3 * j * NSUB + 2] > 0)
+        @pl.when(idx_ref[3 * (base + j * NSUB) + 2] > 0)
         def _():
             for k in range(j * NSUB, (j + 1) * NSUB):
                 body(k)
 
 
-def _fwd_kernel(base, idx_ref, h_ref, w_hbm, hout_ref, y_ref, w_vmem, sems):
+def _fwd_kernel(base, layer, at_ref, idx_ref, h_ref, w_hbm, sh_in, sy_in, hout_ref, sh_ref, sy_ref, w_vmem, y_vmem, sems, io_sems):
+    del sh_in, sy_in
     width = h_ref.shape[1]
+    at = at_ref[0]
     copies = _w_copies(w_hbm, base, w_vmem, sems)
-    y_ref[...] = jnp.zeros_like(y_ref)
+    save_h = pltpu.make_async_copy(h_ref, sh_ref.at[at, layer], io_sems.at[0])
+    save_h.start()
+    y_vmem[...] = jnp.zeros_like(y_vmem)
 
     def body(k):
-        r = idx_ref[3 * k]
-        c = idx_ref[3 * k + 1]
+        r = idx_ref[3 * (base + k)]
+        c = idx_ref[3 * (base + k) + 1]
         p = jnp.dot(h_ref[:, _blk(r)], w_vmem[k], preferred_element_type=jnp.float32)
-        y_ref[:, _blk(c)] += p * _flag(idx_ref, k)
-
-    _slot_chunks(idx_ref, copies, body)
+        y_vmem[:, _blk(c)] += p * _flag(idx_ref, base + k)
+
+    _slot_chunks(idx_ref, base, copies, body)
+    save_y = pltpu.make_async_copy(y_vmem, sy_ref.at[at, layer], io_sems.at[1])
+    save_y.start()
 
     def epi(j, carry):
-        y = y_ref[:, _chunk(j)]
+        y = y_vmem[:, _chunk(j)]
         h = h_ref[:, _chunk(j)].astype(jnp.float32)
         hout_ref[:, _chunk(j)] = (h + y / (1.0 + jnp.exp(-y))).astype(hout_ref.dtype)
         return carry
 
     lax.fori_loop(0, width // CH, epi, 0)
-
-
-def layer_forward(h, weights, layer, il):
+    save_h.wait()
+    save_y.wait()
+
+
+def layer_forward(h, weights, layer, block_index, at, stash_h, stash_y):
     rows, width = h.shape
     return pl.pallas_call(
-        functools.partial(_fwd_kernel, layer * KMAX),
+        functools.partial(_fwd_kernel, layer * KMAX, layer),
         out_shape=(
             jax.ShapeDtypeStruct((rows, width), jnp.bfloat16),
-            jax.ShapeDtypeStruct((rows, width), jnp.float32),
+            jax.ShapeDtypeStruct(stash_h.shape, stash_h.dtype),
+            jax.ShapeDtypeStruct(stash_y.shape, stash_y.dtype),
         ),
-        in_specs=[_SMEM, _VMEM, _ANY],
-        out_specs=(_VMEM, _VMEM),
+        in_specs=[_SMEM, _SMEM, _VMEM, _ANY, _ANY, _ANY],
+        out_specs=(_VMEM, _ANY, _ANY),
         scratch_shapes=[
             pltpu.VMEM((KMAX, BLK, BLK), weights.dtype),
+            pltpu.VMEM((rows, width), jnp.float32),
             pltpu.SemaphoreType.DMA((KMAX // NSUB,)),
+            pltpu.SemaphoreType.DMA((2,)),
         ],
+        input_output_aliases={4: 1, 5: 2},
         compiler_params=pltpu.CompilerParams(vmem_limit_bytes=VMEM_LIMIT),
-    )(il.reshape(-1), h, weights)
-
-
-def _bwd_kernel(base, idx_ref, g_ref, y_ref, w_hbm, gout_ref, s_ref, sp_ref, w_vmem, sems):
+    )(at.reshape(1), block_index.reshape(-1), h, weights, stash_h, stash_y)
+
+
+def _bwd_kernel(base, layer, at_ref, idx_ref, g_ref, sy_hbm, w_hbm, ss_in, gout_ref, ss_ref, y_vmem, s_vmem, sp_ref, w_vmem, sems, io_sems):
+    del ss_in
     width = g_ref.shape[1]
+    at = at_ref[0]
+    load_y = pltpu.make_async_copy(sy_hbm.at[at, layer], y_vmem, io_sems.at[0])
+    load_y.start()
     copies = _w_copies(w_hbm, base, w_vmem, sems)
+    load_y.wait()
 
     def pre(j, carry):
-        y = y_ref[:, _chunk(j)]
+        y = y_vmem[:, _chunk(j)]
         sig = 1.0 / (1.0 + jnp.exp(-y))
         g = g_ref[:, _chunk(j)].astype(jnp.float32)
-        s_ref[:, _chunk(j)] = (g * sig * (1.0 + y * (1.0 - sig))).astype(s_ref.dtype)
+        s_vmem[:, _chunk(j)] = (g * sig * (1.0 + y * (1.0 - sig))).astype(s_vmem.dtype)
         sp_ref[:, _chunk(j)] = jnp.zeros((g_ref.shape[0], CH), jnp.float32)
         return carry
 
     lax.fori_loop(0, width // CH, pre, 0)
+    save_s = pltpu.make_async_copy(s_vmem, ss_ref.at[at, layer], io_sems.at[1])
+    save_s.start()
 
     def body(k):
-        r = idx_ref[3 * k]
-        c = idx_ref[3 * k + 1]
+        r = idx_ref[3 * (base + k)]
+        c = idx_ref[3 * (base + k) + 1]
         back = lax.dot_general(
-            s_ref[:, _blk(c)],
+            s_vmem[:, _blk(c)],
             w_vmem[k],
             (((1,), (1,)), ((), ())),
             preferred_element_type=jnp.float32,
         )
-        sp_ref[:, _blk(r)] += back * _flag(idx_ref, k)
-
-    _slot_chunks(idx_ref, copies, body)
+        sp_ref[:, _blk(r)] += back * _flag(idx_ref, base + k)
+
+    _slot_chunks(idx_ref, base, copies, body)
 
     def epi(j, carry):
         g = g_ref[:, _chunk(j)].astype(jnp.float32)
@@ -131,25 +150,30 @@
         return carry
 
     lax.fori_loop(0, width // CH, epi, 0)
-
-
-def layer_backward(g, y, weights, layer, il):
+    save_s.wait()
+
+
+def layer_backward(g, stash_y, weights, layer, block_index, at, stash_s):
     rows, width = g.shape
     return pl.pallas_call(
-        functools.partial(_bwd_kernel, layer * KMAX),
+        functools.partial(_bwd_kernel, layer * KMAX, layer),
         out_shape=(
             jax.ShapeDtypeStruct((rows, width), jnp.bfloat16),
-            jax.ShapeDtypeStruct((rows, width), jnp.bfloat16),
+            jax.ShapeDtypeStruct(stash_s.shape, stash_s.dtype),
         ),
-        in_specs=[_SMEM, _VMEM, _VMEM, _ANY],
-        out_specs=(_VMEM, _VMEM),
+        in_specs=[_SMEM, _SMEM, _VMEM, _ANY, _ANY, _ANY],
+        out_specs=(_VMEM, _ANY),
         scratch_shapes=[
+            pltpu.VMEM((rows, width), jnp.float32),
+            pltpu.VMEM((rows, width), jnp.bfloat16),
             pltpu.VMEM((rows, width), jnp.float32),
             pltpu.VMEM((KMAX, BLK, BLK), weights.dtype),
             pltpu.SemaphoreType.DMA((KMAX // NSUB,)),
+            pltpu.SemaphoreType.DMA((2,)),
         ],
+        input_output_aliases={5: 1},
         compiler_params=pltpu.CompilerParams(vmem_limit_bytes=VMEM_LIMIT),
-    )(il.reshape(-1), g, y, weights)
+    )(at.reshape(1), block_index.reshape(-1), g, stash_y, weights, stash_s)
 
 
 def _dw_kernel(mbs, idx_ref, h_ref, s_ref, dw_ref):
@@ -218,27 +242,6 @@
     idx = block_index.reshape(LSLOT, KMAX, 3)
     ticks = mbs + segments - 1
 
-    def segment_forward(start):
-        h = start
-        inputs = []
-        preacts = []
-        for layer in range(LSLOT):
-            h_next, y = layer_forward(h, weights, layer, idx[layer])
-            inputs.append(h)
-            preacts.append(y)
-            h = h_next
-        return (h, jnp.stack(inputs), jnp.stack(preacts))
-
-    def skip_forward(start):
-        return (
-            start,
-            jnp.zeros((LSLOT, rows_dev, width), jnp.bfloat16),
-            jnp.zeros((LSLOT, rows_dev, width), jnp.float32),
-        )
-
-    stash_h = jnp.zeros((mbs + 1, LSLOT, rows_dev, width), jnp.bfloat16)
-    stash_y = jnp.zeros((mbs + 1, LSLOT, rows_dev, width), jnp.float32)
-
     def forward_tick(tick, carry):
         received, saved_h, saved_y = carry
         micro = tick - me_segment
@@ -246,18 +249,24 @@
         place_at = jnp.clip(micro, 0, mbs - 1)
         first = lax.dynamic_index_in_dim(x_in, place_at, 0, keepdims=False)
         start = jnp.where(me_segment == 0, first, received)
-        h_out, inputs, preacts = lax.cond(live, segment_forward, skip_forward, start)
-        store_at = jnp.where(live, place_at, mbs)
-        saved_h = lax.dynamic_update_index_in_dim(saved_h, inputs, store_at, 0)
-        saved_y = lax.dynamic_update_index_in_dim(saved_y, preacts, store_at, 0)
+
+        def run(operands):
+            h, sh, sy = operands
+            for layer in range(LSLOT):
+                h, sh, sy = layer_forward(h, weights, layer, block_index, place_at, sh, sy)
+            return (h, sh, sy)
+
+        h_out, saved_h, saved_y = lax.cond(live, run, lambda ops: ops, (start, saved_h, saved_y))
         received = shifted(h_out, "segment", 1)
         return (received, saved_h, saved_y)
 
+    stash_h = jnp.zeros((mbs, LSLOT, rows_dev, width), jnp.bfloat16)
+    stash_y = jnp.zeros((mbs, LSLOT, rows_dev, width), jnp.float32)
     blank = jnp.zeros((rows_dev, width), jnp.bfloat16)
     unused_recv, stash_h, stash_y = lax.fori_loop(
         0, ticks, forward_tick, (blank, stash_h, stash_y)
     )
-    stash_s = jnp.zeros((mbs + 1, LSLOT, rows_dev, width), jnp.bfloat16)
+    stash_s = jnp.zeros((mbs, LSLOT, rows_dev, width), jnp.bfloat16)
 
     def backward_tick(tick, carry):
         received, saved_s = carry
@@ -266,19 +275,14 @@
         place_at = jnp.clip(micro, 0, mbs - 1)
         top = lax.dynamic_index_in_dim(cotangent, place_at, 0, keepdims=False)
         grad_in = jnp.where(me_segment == segments - 1, top, received)
-        layer_y = lax.dynamic_index_in_dim(stash_y, place_at, 0, keepdims=False)
-
-        def run_back(grad):
-            s_parts = [None] * LSLOT
+
+        def run(operands):
+            grad, ss = operands
             for layer in reversed(range(LSLOT)):
-                grad, s_parts[layer] = layer_backward(grad, layer_y[layer], weights, layer, idx[layer])
-            return (grad, jnp.stack(s_parts))
-
-        def skip_back(grad):
-            return (grad, jnp.zeros((LSLOT, rows_dev, width), jnp.bfloat16))
-
-        grad_out, s_all = lax.cond(live, run_back, skip_back, grad_in)
-        saved_s = lax.dynamic_update_index_in_dim(saved_s, s_all, jnp.where(live, place_at, mbs), 0)
+                grad, ss = layer_backward(grad, stash_y, weights, layer, block_index, place_at, ss)
+            return (grad, ss)
+
+        grad_out, saved_s = lax.cond(live, run, lambda ops: ops, (grad_in, saved_s))
         received = shifted(grad_out, "segment", -1)
         return (received, saved_s)
 

time: 568 us -> 498 us (0.88)
  local copies, waits for them, and re-layouts: 92.9 us -> 25.7 us
  waiting for transfers between devices: 304 us -> 321 us
  other arithmetic: 41.8 us -> 28.5 us
  starting transfers between devices: 61.5 us -> 49.2 us
  Pallas kernels: 66 us -> 71.7 us
    dynamic_update_slice x15 -> x0, local copies, waits for them, and re-layouts: 37.6 us -> none  [the longest x5 22.8 us: forward_tick(): saved_y = lax.dynamic_update_index_in_dim(saved_y, preacts, store_at, 0)]
    ppermute x10, waiting for transfers between devices: 256 us -> 272 us  [shifted(): lax.ppermute(value, axis, [(source, source + steps) for source in range(l...]
    squeeze x10 -> x0, local copies, waits for them, and re-layouts: 15.7 us -> none  [the longest x2 9.33 us: run_back(): layer_y[layer]]
    ppermute x10, starting transfers between devices: 61.4 us -> 49.1 us  [shifted(): lax.ppermute(value, axis, [(source, source + steps) for source in range(l...]
    broadcast_in_dim x6 -> x0, other arithmetic: 11.7 us -> none  [the longest x2 7.85 us: forward_tick(): saved_y = lax.dynamic_update_index_in_dim(saved_y, preacts, store_at, 0)]
    broadcast_in_dim x10 -> x1, local copies, waits for them, and re-layouts: 14.4 us -> 4.21 us  [on_device(): stash_y = jnp.zeros((mbs, LSLOT, rows_dev, width), jnp.float32)]
    pallas_call x8, Pallas kernels: 50.3 us -> 56.3 us  [the longest x4 32.9 us: layer_backward(): pl.pallas_call(functools.partial(_bwd_kernel, layer * KMAX, layer), out_s...]
  transfers between devices with their start and end apart: 13 -> 13, of which waited for: 13 -> 13; matrix products, arithmetic and copies ran while one was open for 7% -> 0% of each run, Pallas kernels for 0% -> 0%
where the time goes in v2:
time: 498 us; the launch traced here: 496 us
  waiting for transfers between devices  321 us (64%)
  Pallas kernels  71.7 us (14%)
  starting transfers between devices  49.2 us (10%)
  other arithmetic  28.5 us (6%)
  local copies, waits for them, and re-layouts  25.7 us (5%)
    ppermute x10, waiting for transfers between devices, shifted(): lax.ppermute(value, axis, [(source, source + steps) for source in range(l...  272 us
    ppermute x10, starting transfers between devices, shifted(): lax.ppermute(value, axis, [(source, source + steps) for source in range(l...  49.1 us
    ppermute x3, waiting for transfers between devices, _exchange(): lax.ppermute(send.astype(jnp.bfloat16), 'dp', pairs).astype(jnp.float32)  48.4 us
    pallas_call x4, Pallas kernels, layer_backward(): pl.pallas_call(functools.partial(_bwd_kernel, layer * KMAX, layer), out_s...  32.9 us
    pallas_call x4, Pallas kernels, layer_forward(): pl.pallas_call(functools.partial(_fwd_kernel, layer * KMAX, layer), out_s...  23.5 us
    pallas_call x1, Pallas kernels, segment_dw(): pl.pallas_call(functools.partial(_dw_kernel, mbs), out_shape=jax.ShapeDty...  15.4 us
  transfers between devices with their start and end apart: 13, of which 13 were waited for; matrix products, arithmetic and copies ran while one was open for 0% of the time, Pallas kernels for 0%

profile of v2, /device:TPU:0, one launch (start us, length us, event | category | flops | bytes accessed | tf_op | source)
XLA Modules:
  0.0 496.3 jit_solution(16027363912679164608)
XLA Ops:
  1.6 4.2 broadcast_in_dim.7
  5.8 2.4 broadcast.7.clone
  8.3 182.2 %while.35 = (s32[]{:T(128)}, bf16[64,8192]{1,0:T(8,128)(2,1)S(1)}, bf16[2,2,64,8192]{3,2,1,0:T(8,128)(2,1)}, f32[2,2,64,8192]{3,2,1,0:T(8,128)}, s32[]{:T(128)},...) while((s32[]{:T(128)}, bf16[64,8192]{1,0:T(8,128)(2,1)S(1)}, ...), condition=%wide.region_3.4_spmd, body=%wide.region_0.3_spmd.sunk | while | flops 524297 | bytes 7346480 | solution.py:266
  8.4 1.3 bitcast_select_fusion.6
  9.7 12.5 %conditional.4 = ((bf16[64,8192]{1,0:T(8,128)(2,1)S(1)}, bf16[2,2,64,8192]{3,2,1,0:T(8,128)(2,1)}, f32[2,2,64,8192]{3,2,1,0:T(8,128)})) conditional(s32[]{:T(128)} %convert_element_type.61, (bf16[64,8192]{1,0:T(8,128)(2,1)S(1)}, bf16[2,2,64,8192]{3,2,1,0:T(8,128)(2,1)}, f32[2,2,64,8192]{3,2,1,0:T(8,128)}) %tuple.81, (s32[]{:T(128)}, ...), branch_computations={%region_1.1_spmd, %region_2.2_spmd} | conditional | bytes 6152 | solution.py:259
  10.5 5.9 %branch_1_fun.4 = (bf16[64,8192]{1,0:T(8,128)(2,1)}, bf16[2,2,64,8192]{3,2,1,0:T(8,128)(2,1)}, f32[2,2,64,8192]{3,2,1,0:T(8,128)}) custom-call(s32[1]{0:T(128)} %bitcast.at_ref, s32[768]{0:T(1024)} %reshape.17.idx_ref, bf16[64,8192]{1,0:T(8,128)(2,1)S(1)} %get-tuple-element.401.h_ref, ...), custom_call_target="tpu_custom_call", output_to_operand_aliasing={{1}: (4, {}), {2}: (5, {})} | custom-call | tf_op jit(solution)/shard_map/while/body/eval_jaxpr/cond/branch_1_fun/pallas_call | solution.py:93
  16.5 5.8 %branch_1_fun.5 = (bf16[64,8192]{1,0:T(8,128)(2,1)S(1)}, bf16[2,2,64,8192]{3,2,1,0:T(8,128)(2,1)}, f32[2,2,64,8192]{3,2,1,0:T(8,128)}) custom-call(s32[1]{0:T(128)} %bitcast.at_ref, s32[768]{0:T(1024)} %reshape.17.idx_ref, bf16[64,8192]{1,0:T(8,128)(2,1)} %get-tuple-element.405.h_ref, ...), custom_call_target="tpu_custom_call", output_to_operand_aliasing={{1}: (4, {}), {2}: (5, {})} | custom-call | tf_op jit(solution)/shard_map/while/body/eval_jaxpr/cond/branch_1_fun/pallas_call | solution.py:93
  22.3 1.4 collective-permute-start
  23.6 23.2 %collective-permute-done = bf16[64,8192]{1,0:T(8,128)(2,1)S(1)} collective-permute-done((bf16[64,8192]{1,0:T(8,128)(2,1)S(1)}, bf16[64,8192]{1,0:T(8,128)(2,1)S(1)}, u32[]{:S(2)}, u32[]{:S(2)}) %collective-permute-start) | collective-permute-done | bytes 1048608 | tf_op jit(solution)/shard_map/while/body/eval_jaxpr/ppermute | solution.py:25
  48.2 12.6 %conditional.4 = ((bf16[64,8192]{1,0:T(8,128)(2,1)S(1)}, bf16[2,2,64,8192]{3,2,1,0:T(8,128)(2,1)}, f32[2,2,64,8192]{3,2,1,0:T(8,128)})) conditional(s32[]{:T(128)} %convert_element_type.61, (bf16[64,8192]{1,0:T(8,128)(2,1)S(1)}, bf16[2,2,64,8192]{3,2,1,0:T(8,128)(2,1)}, f32[2,2,64,8192]{3,2,1,0:T(8,128)}) %tuple.81, (s32[]{:T(128)}, ...), branch_computations={%region_1.1_spmd, %region_2.2_spmd} | conditional | bytes 6152 | solution.py:259
  49.0 6.0 %branch_1_fun.4 = (bf16[64,8192]{1,0:T(8,128)(2,1)}, bf16[2,2,64,8192]{3,2,1,0:T(8,128)(2,1)}, f32[2,2,64,8192]{3,2,1,0:T(8,128)}) custom-call(s32[1]{0:T(128)} %bitcast.at_ref, s32[768]{0:T(1024)} %reshape.17.idx_ref, bf16[64,8192]{1,0:T(8,128)(2,1)S(1)} %get-tuple-element.401.h_ref, ...), custom_call_target="tpu_custom_call", output_to_operand_aliasing={{1}: (4, {}), {2}: (5, {})} | custom-call | tf_op jit(solution)/shard_map/while/body/eval_jaxpr/cond/branch_1_fun/pallas_call | solution.py:93
  55.0 5.8 %branch_1_fun.5 = (bf16[64,8192]{1,0:T(8,128)(2,1)S(1)}, bf16[2,2,64,8192]{3,2,1,0:T(8,128)(2,1)}, f32[2,2,64,8192]{3,2,1,0:T(8,128)}) custom-call(s32[1]{0:T(128)} %bitcast.at_ref, s32[768]{0:T(1024)} %reshape.17.idx_ref, bf16[64,8192]{1,0:T(8,128)(2,1)} %get-tuple-element.405.h_ref, ...), custom_call_target="tpu_custom_call", output_to_operand_aliasing={{1}: (4, {}), {2}: (5, {})} | custom-call | tf_op jit(solution)/shard_map/while/body/eval_jaxpr/cond/branch_1_fun/pallas_call | solution.py:93
  60.8 5.0 %collective-permute-start = (bf16[64,8192]{1,0:T(8,128)(2,1)S(1)}, bf16[64,8192]{1,0:T(8,128)(2,1)S(1)}, u32[]{:S(2)}, u32[]{:S(2)}) collective-permute-start(bf16[64,8192]{1,0:T(8,128)(2,1)S(1)} %get-tuple-element.625), channel_id=1, source_target_pairs={{0,8},{8,16},{16,24},{1,9},{9,17},{17,25},{2,10},{10,18},{18,26},{... | collective-permute-start | bytes 3145736 | tf_op jit(solution)/shard_map/while/body/eval_jaxpr/ppermute | solution.py:25
  65.8 22.4 %collective-permute-done = bf16[64,8192]{1,0:T(8,128)(2,1)S(1)} collective-permute-done((bf16[64,8192]{1,0:T(8,128)(2,1)S(1)}, bf16[64,8192]{1,0:T(8,128)(2,1)S(1)}, u32[]{:S(2)}, u32[]{:S(2)}) %collective-permute-start) | collective-permute-done | bytes 1048608 | tf_op jit(solution)/shard_map/while/body/eval_jaxpr/ppermute | solution.py:25
  89.5 17.6 %collective-permute-start = (bf16[64,8192]{1,0:T(8,128)(2,1)S(1)}, bf16[64,8192]{1,0:T(8,128)(2,1)S(1)}, u32[]{:S(2)}, u32[]{:S(2)}) collective-permute-start(bf16[64,8192]{1,0:T(8,128)(2,1)S(1)} %get-tuple-element.625), channel_id=1, source_target_pairs={{0,8},{8,16},{16,24},{1,9},{9,17},{17,25},{2,10},{10,18},{18,26},{... | collective-permute-start | bytes 3145736 | tf_op jit(solution)/shard_map/while/body/eval_jaxpr/ppermute | solution.py:25
  107.1 21.5 %collective-permute-done = bf16[64,8192]{1,0:T(8,128)(2,1)S(1)} collective-permute-done((bf16[64,8192]{1,0:T(8,128)(2,1)S(1)}, bf16[64,8192]{1,0:T(8,128)(2,1)S(1)}, u32[]{:S(2)}, u32[]{:S(2)}) %collective-permute-start) | collective-permute-done | bytes 1048608 | tf_op jit(solution)/shard_map/while/body/eval_jaxpr/ppermute | solution.py:25
  130.0 4.5 collective-permute-start
  134.5 20.6 %collective-permute-done = bf16[64,8192]{1,0:T(8,128)(2,1)S(1)} collective-permute-done((bf16[64,8192]{1,0:T(8,128)(2,1)S(1)}, bf16[64,8192]{1,0:T(8,128)(2,1)S(1)}, u32[]{:S(2)}, u32[]{:S(2)}) %collective-permute-start) | collective-permute-done | bytes 1048608 | tf_op jit(solution)/shard_map/while/body/eval_jaxpr/ppermute | solution.py:25
  156.4 14.2 %collective-permute-start = (bf16[64,8192]{1,0:T(8,128)(2,1)S(1)}, bf16[64,8192]{1,0:T(8,128)(2,1)S(1)}, u32[]{:S(2)}, u32[]{:S(2)}) collective-permute-start(bf16[64,8192]{1,0:T(8,128)(2,1)S(1)} %get-tuple-element.625), channel_id=1, source_target_pairs={{0,8},{8,16},{16,24},{1,9},{9,17},{17,25},{2,10},{10,18},{18,26},{... | collective-permute-start | bytes 3145736 | tf_op jit(solution)/shard_map/while/body/eval_jaxpr/ppermute | solution.py:25
  170.6 19.9 %collective-permute-done = bf16[64,8192]{1,0:T(8,128)(2,1)S(1)} collective-permute-done((bf16[64,8192]{1,0:T(8,128)(2,1)S(1)}, bf16[64,8192]{1,0:T(8,128)(2,1)S(1)}, u32[]{:S(2)}, u32[]{:S(2)}) %collective-permute-start) | collective-permute-done | bytes 1048608 | tf_op jit(solution)/shard_map/while/body/eval_jaxpr/ppermute | solution.py:25
  190.6 2.5 broadcast.7
  193.1 212.4 %while.36 = (s32[]{:T(128)}, bf16[64,8192]{1,0:T(8,128)(2,1)S(1)}, bf16[2,2,64,8192]{3,2,1,0:T(8,128)(2,1)}, s32[]{:T(128)}, pred[]{:T(512)}, /*index=5*/bf16[2,...) while((s32[]{:T(128)}, bf16[64,8192]{1,0:T(8,128)(2,1)S(1)}, ...), condition=%wide.region_7.8_spmd, body=%wide.region_4.7_spmd.sunk | while | flops 524297 | bytes 7346472 | solution.py:289
  193.1 1.3 bitcast_select_fusion.7
  195.8 22.9 %collective-permute-done.1 = bf16[64,8192]{1,0:T(8,128)(2,1)S(1)} collective-permute-done((bf16[64,8192]{1,0:T(8,128)(2,1)S(1)}, bf16[64,8192]{1,0:T(8,128)(2,1)S(1)}, u32[]{:S(2)}, u32[]{:S(2)}) %collective-permute-start.1) | collective-permute-done | bytes 1048608 | tf_op jit(solution)/shard_map/while/body/eval_jaxpr/ppermute | solution.py:25
  218.7 1.3 bitcast_select_fusion.7
  221.4 32.6 %collective-permute-done.1 = bf16[64,8192]{1,0:T(8,128)(2,1)S(1)} collective-permute-done((bf16[64,8192]{1,0:T(8,128)(2,1)S(1)}, bf16[64,8192]{1,0:T(8,128)(2,1)S(1)}, u32[]{:S(2)}, u32[]{:S(2)}) %collective-permute-start.1) | collective-permute-done | bytes 1048608 | tf_op jit(solution)/shard_map/while/body/eval_jaxpr/ppermute | solution.py:25
  253.9 1.3 bitcast_select_fusion.7
  256.6 68.3 %collective-permute-done.1 = bf16[64,8192]{1,0:T(8,128)(2,1)S(1)} collective-permute-done((bf16[64,8192]{1,0:T(8,128)(2,1)S(1)}, bf16[64,8192]{1,0:T(8,128)(2,1)S(1)}, u32[]{:S(2)}, u32[]{:S(2)}) %collective-permute-start.1) | collective-permute-done | bytes 1048608 | tf_op jit(solution)/shard_map/while/body/eval_jaxpr/ppermute | solution.py:25
  324.9 1.3 bitcast_select_fusion.7
  326.3 17.2 %conditional.5 = ((bf16[64,8192]{1,0:T(8,128)(2,1)S(1)}, bf16[2,2,64,8192]{3,2,1,0:T(8,128)(2,1)})) conditional(s32[]{:T(128)} %convert_element_type.62, (bf16[64,8192]{1,0:T(8,128)(2,1)S(1)}, bf16[2,2,64,8192]{3,2,1,0:T(8,128)(2,1)}) %tuple.84, (s32[]{:T(128)}, s32[256,3]{1,0:T(8,128)S(1)}, bf16[64,8192]{1,0:T(8,128)(2,1)S(1)}, ...), branch_computations={%region_5.5_spmd, %region_6.6_spmd} | conditional | bytes 6152 | solution.py:285
  327.1 8.7 %branch_1_fun.6 = (bf16[64,8192]{1,0:T(8,128)(2,1)}, bf16[2,2,64,8192]{3,2,1,0:T(8,128)(2,1)}) custom-call(s32[1]{0:T(128)} %bitcast.2.at_ref, s32[768]{0:T(1024)} %reshape.21.idx_ref, bf16[64,8192]{1,0:T(8,128)(2,1)S(1)} %get-tuple-element.423.g_ref, f32[2,2,64,8192]{3,2,1,0:T(8,128)} %get-tuple-element.424.sy_hbm, ...), custom_call_target="tpu_custom_call", output_to_operand_aliasing={{1}: (5, {})} | custom-call | tf_op jit(solution)/shard_map/while/body/eval_jaxpr/cond/branch_1_fun/pallas_call | solution.py:158
  335.8 7.8 %branch_1_fun.7 = (bf16[64,8192]{1,0:T(8,128)(2,1)S(1)}, bf16[2,2,64,8192]{3,2,1,0:T(8,128)(2,1)}) custom-call(s32[1]{0:T(128)} %bitcast.2.at_ref, s32[768]{0:T(1024)} %reshape.21.idx_ref, bf16[64,8192]{1,0:T(8,128)(2,1)} %get-tuple-element.427.g_ref, f32[2,2,64,8192]{3,2,1,0:T(8,128)} %get-tuple-element.424.sy_hbm, ...), custom_call_target="tpu_custom_call", output_to_operand_aliasing={{1}: (5, {})} | custom-call | tf_op jit(solution)/shard_map/while/body/eval_jaxpr/cond/branch_1_fun/pallas_call | solution.py:158
  344.8 21.2 %collective-permute-done.1 = bf16[64,8192]{1,0:T(8,128)(2,1)S(1)} collective-permute-done((bf16[64,8192]{1,0:T(8,128)(2,1)S(1)}, bf16[64,8192]{1,0:T(8,128)(2,1)S(1)}, u32[]{:S(2)}, u32[]{:S(2)}) %collective-permute-start.1) | collective-permute-done | bytes 1048608 | tf_op jit(solution)/shard_map/while/body/eval_jaxpr/ppermute | solution.py:25
  366.0 1.3 bitcast_select_fusion.7
  367.3 17.2 %conditional.5 = ((bf16[64,8192]{1,0:T(8,128)(2,1)S(1)}, bf16[2,2,64,8192]{3,2,1,0:T(8,128)(2,1)})) conditional(s32[]{:T(128)} %convert_element_type.62, (bf16[64,8192]{1,0:T(8,128)(2,1)S(1)}, bf16[2,2,64,8192]{3,2,1,0:T(8,128)(2,1)}) %tuple.84, (s32[]{:T(128)}, s32[256,3]{1,0:T(8,128)S(1)}, bf16[64,8192]{1,0:T(8,128)(2,1)S(1)}, ...), branch_computations={%region_5.5_spmd, %region_6.6_spmd} | conditional | bytes 6152 | solution.py:285
  368.1 8.7 %branch_1_fun.6 = (bf16[64,8192]{1,0:T(8,128)(2,1)}, bf16[2,2,64,8192]{3,2,1,0:T(8,128)(2,1)}) custom-call(s32[1]{0:T(128)} %bitcast.2.at_ref, s32[768]{0:T(1024)} %reshape.21.idx_ref, bf16[64,8192]{1,0:T(8,128)(2,1)S(1)} %get-tuple-element.423.g_ref, f32[2,2,64,8192]{3,2,1,0:T(8,128)} %get-tuple-element.424.sy_hbm, ...), custom_call_target="tpu_custom_call", output_to_operand_aliasing={{1}: (5, {})} | custom-call | tf_op jit(solution)/shard_map/while/body/eval_jaxpr/cond/branch_1_fun/pallas_call | solution.py:158
  376.8 7.8 %branch_1_fun.7 = (bf16[64,8192]{1,0:T(8,128)(2,1)S(1)}, bf16[2,2,64,8192]{3,2,1,0:T(8,128)(2,1)}) custom-call(s32[1]{0:T(128)} %bitcast.2.at_ref, s32[768]{0:T(1024)} %reshape.21.idx_ref, bf16[64,8192]{1,0:T(8,128)(2,1)} %get-tuple-element.427.g_ref, f32[2,2,64,8192]{3,2,1,0:T(8,128)} %get-tuple-element.424.sy_hbm, ...), custom_call_target="tpu_custom_call", output_to_operand_aliasing={{1}: (5, {})} | custom-call | tf_op jit(solution)/shard_map/while/body/eval_jaxpr/cond/branch_1_fun/pallas_call | solution.py:158
  385.9 19.6 %collective-permute-done.1 = bf16[64,8192]{1,0:T(8,128)(2,1)S(1)} collective-permute-done((bf16[64,8192]{1,0:T(8,128)(2,1)S(1)}, bf16[64,8192]{1,0:T(8,128)(2,1)S(1)}, u32[]{:S(2)}, u32[]{:S(2)}) %collective-permute-start.1) | collective-permute-done | bytes 1048608 | tf_op jit(solution)/shard_map/while/body/eval_jaxpr/ppermute | solution.py:25
  405.5 15.4 %shard_map.46 = f32[256,128,128]{2,1,0:T(8,128)} custom-call(s32[768]{0:T(1024)} %reshape.24.idx_ref, bf16[2,2,64,8192]{3,2,1,0:T(8,128)(2,1)} %get-tuple-element.444.h_ref, bf16[2,2,64,8192]{3,2,1,0:T(8,128)(2,1)} %get-tuple-element.446.s_ref), custom_call_target="tpu_custom_call" | custom-call | tf_op jit(solution)/shard_map/pallas_call | solution.py:205
  420.9 6.4 %fusion = bf16[2,2,32,128,128]{4,3,2,1,0:T(8,128)(2,1)} fusion(f32[2,2,2,32,128,128]{5,4,3,2,1,0:T(8,128)} %bitcast.31, s32[]{:T(128)S(6)} %select_n.107), kind=kLoop, calls=%fused_computation.4 | loop fusion | bytes 8388612 | tf_op jit(solution)/shard_map/convert_element_type | solution.py:215
  427.2 7.5 %collective-permute-done.2 = bf16[2,2,32,128,128]{4,3,2,1,0:T(8,128)(2,1)} collective-permute-done((bf16[2,2,32,128,128]{4,3,2,1,0:T(8,128)(2,1)}, bf16[2,2,32,128,128]{4,3,2,1,0:T(8,128)(2,1)}, u32[]{:S(2)}, u32[]{:S(2)}) %collective-permute-start.2) | collective-permute-done | bytes 4194336 | tf_op jit(solution)/shard_map/ppermute | solution.py:215
  434.7 5.9 %bitcast_add_fusion = f32[2,2,32,128,128]{4,3,2,1,0:T(8,128)S(1)} fusion(bf16[2,2,32,128,128]{4,3,2,1,0:T(8,128)(2,1)} %collective-permute-done.2, f32[2,2,2,32,128,128]{5,4,3,2,1,0:T(8,128)} %bitcast.32, s32[]{:T(128)S(6)} %select_n.106), kind=kLoop, calls=%fused_computation.2 | loop fusion | flops 4194304 | bytes 20971524 | tf_op jit(solution)/shard_map/add | solution.py:228
  440.7 3.2 copy-done
  444.4 26.1 %collective-permute-done.3 = bf16[2,32,128,128]{3,2,1,0:T(8,128)(2,1)} collective-permute-done((bf16[2,32,128,128]{3,2,1,0:T(8,128)(2,1)S(1)}, bf16[2,32,128,128]{3,2,1,0:T(8,128)(2,1)}, u32[]{:S(2)}, u32[]{:S(2)}) %collective-permute-start.3) | collective-permute-done | bytes 2097184 | tf_op jit(solution)/shard_map/ppermute | solution.py:215
  470.5 5.6 %fusion.2 = f32[2,32,128,128]{3,2,1,0:T(8,128)S(1)} fusion(bf16[2,32,128,128]{3,2,1,0:T(8,128)(2,1)} %collective-permute-done.3, f32[2,2,32,128,128]{4,3,2,1,0:T(8,128)} %copy-done, s32[]{:T(128)S(6)} %select_n.112, s32[]{:T(128)S(6)} %select_n.110, pred[]{:T(512)S(6)} %eq.24), kind=kLoop, calls=%fused_computation.8 | loop fusion | flops 3145728 | bytes 14680073 | tf_op jit(solution)/shard_map/add | solution.py:232
  476.1 2.0 copy-done.1
  478.3 14.8 %collective-permute-done.4 = bf16[32,128,128]{2,1,0:T(8,128)(2,1)S(1)} collective-permute-done((bf16[32,128,128]{2,1,0:T(8,128)(2,1)S(1)}, bf16[32,128,128]{2,1,0:T(8,128)(2,1)S(1)}, u32[]{:S(2)}, u32[]{:S(2)}) %collective-permute-start.4) | collective-permute-done | bytes 1048608 | tf_op jit(solution)/shard_map/ppermute | solution.py:215
  493.1 3.3 bitcast_add_fusion.1
  (30 shorter events, 17.5 us)
Async XLA Ops:
  22.3 24.6 %collective-permute-start = (bf16[64,8192]{1,0:T(8,128)(2,1)S(1)}, bf16[64,8192]{1,0:T(8,128)(2,1)S(1)}, u32[]{:S(2)}, u32[]{:S(2)}) collective-permute-start(bf16[64,8192]{1,0:T(8,128)(2,1)S(1)} %get-tuple-element.625), channel_id=1, source_target_pairs={{0,8},{8,16},{16,24},{1,9},{9,17},{17,25},{2,10},{10,18},{18,26},{... | collective-permute-start | bytes 3145736 | tf_op jit(solution)/shard_map/while/body/eval_jaxpr/ppermute | solution.py:25
  60.8 27.4 %collective-permute-start = (bf16[64,8192]{1,0:T(8,128)(2,1)S(1)}, bf16[64,8192]{1,0:T(8,128)(2,1)S(1)}, u32[]{:S(2)}, u32[]{:S(2)}) collective-permute-start(bf16[64,8192]{1,0:T(8,128)(2,1)S(1)} %get-tuple-element.625), channel_id=1, source_target_pairs={{0,8},{8,16},{16,24},{1,9},{9,17},{17,25},{2,10},{10,18},{18,26},{... | collective-permute-start | bytes 3145736 | tf_op jit(solution)/shard_map/while/body/eval_jaxpr/ppermute | solution.py:25
  89.5 39.1 %collective-permute-start = (bf16[64,8192]{1,0:T(8,128)(2,1)S(1)}, bf16[64,8192]{1,0:T(8,128)(2,1)S(1)}, u32[]{:S(2)}, u32[]{:S(2)}) collective-permute-start(bf16[64,8192]{1,0:T(8,128)(2,1)S(1)} %get-tuple-element.625), channel_id=1, source_target_pairs={{0,8},{8,16},{16,24},{1,9},{9,17},{17,25},{2,10},{10,18},{18,26},{... | collective-permute-start | bytes 3145736 | tf_op jit(solution)/shard_map/while/body/eval_jaxpr/ppermute | solution.py:25
  130.0 25.0 %collective-permute-start = (bf16[64,8192]{1,0:T(8,128)(2,1)S(1)}, bf16[64,8192]{1,0:T(8,128)(2,1)S(1)}, u32[]{:S(2)}, u32[]{:S(2)}) collective-permute-start(bf16[64,8192]{1,0:T(8,128)(2,1)S(1)} %get-tuple-element.625), channel_id=1, source_target_pairs={{0,8},{8,16},{16,24},{1,9},{9,17},{17,25},{2,10},{10,18},{18,26},{... | collective-permute-start | bytes 3145736 | tf_op jit(solution)/shard_map/while/body/eval_jaxpr/ppermute | solution.py:25
  156.4 34.2 %collective-permute-start = (bf16[64,8192]{1,0:T(8,128)(2,1)S(1)}, bf16[64,8192]{1,0:T(8,128)(2,1)S(1)}, u32[]{:S(2)}, u32[]{:S(2)}) collective-permute-start(bf16[64,8192]{1,0:T(8,128)(2,1)S(1)} %get-tuple-element.625), channel_id=1, source_target_pairs={{0,8},{8,16},{16,24},{1,9},{9,17},{17,25},{2,10},{10,18},{18,26},{... | collective-permute-start | bytes 3145736 | tf_op jit(solution)/shard_map/while/body/eval_jaxpr/ppermute | solution.py:25
  194.5 24.2 %collective-permute-start.1 = (bf16[64,8192]{1,0:T(8,128)(2,1)S(1)}, bf16[64,8192]{1,0:T(8,128)(2,1)S(1)}, u32[]{:S(2)}, u32[]{:S(2)}) collective-permute-start(bf16[64,8192]{1,0:T(8,128)(2,1)S(1)} %get-tuple-element.637), channel_id=1, source_target_pairs={{8,0},{16,8},{24,16},{9,1},{17,9},{25,17},{10,2},{18,10},{26,18},{... | collective-permute-start | bytes 3145736 | tf_op jit(solution)/shard_map/while/body/eval_jaxpr/ppermute | solution.py:25
  220.1 33.9 %collective-permute-start.1 = (bf16[64,8192]{1,0:T(8,128)(2,1)S(1)}, bf16[64,8192]{1,0:T(8,128)(2,1)S(1)}, u32[]{:S(2)}, u32[]{:S(2)}) collective-permute-start(bf16[64,8192]{1,0:T(8,128)(2,1)S(1)} %get-tuple-element.637), channel_id=1, source_target_pairs={{8,0},{16,8},{24,16},{9,1},{17,9},{25,17},{10,2},{18,10},{26,18},{... | collective-permute-start | bytes 3145736 | tf_op jit(solution)/shard_map/while/body/eval_jaxpr/ppermute | solution.py:25
  255.3 69.6 %collective-permute-start.1 = (bf16[64,8192]{1,0:T(8,128)(2,1)S(1)}, bf16[64,8192]{1,0:T(8,128)(2,1)S(1)}, u32[]{:S(2)}, u32[]{:S(2)}) collective-permute-start(bf16[64,8192]{1,0:T(8,128)(2,1)S(1)} %get-tuple-element.637), channel_id=1, source_target_pairs={{8,0},{16,8},{24,16},{9,1},{17,9},{25,17},{10,2},{18,10},{26,18},{... | collective-permute-start | bytes 3145736 | tf_op jit(solution)/shard_map/while/body/eval_jaxpr/ppermute | solution.py:25
  343.5 22.5 %collective-permute-start.1 = (bf16[64,8192]{1,0:T(8,128)(2,1)S(1)}, bf16[64,8192]{1,0:T(8,128)(2,1)S(1)}, u32[]{:S(2)}, u32[]{:S(2)}) collective-permute-start(bf16[64,8192]{1,0:T(8,128)(2,1)S(1)} %get-tuple-element.637), channel_id=1, source_target_pairs={{8,0},{16,8},{24,16},{9,1},{17,9},{25,17},{10,2},{18,10},{26,18},{... | collective-permute-start | bytes 3145736 | tf_op jit(solution)/shard_map/while/body/eval_jaxpr/ppermute | solution.py:25
  384.6 20.9 %collective-permute-start.1 = (bf16[64,8192]{1,0:T(8,128)(2,1)S(1)}, bf16[64,8192]{1,0:T(8,128)(2,1)S(1)}, u32[]{:S(2)}, u32[]{:S(2)}) collective-permute-start(bf16[64,8192]{1,0:T(8,128)(2,1)S(1)} %get-tuple-element.637), channel_id=1, source_target_pairs={{8,0},{16,8},{24,16},{9,1},{17,9},{25,17},{10,2},{18,10},{26,18},{... | collective-permute-start | bytes 3145736 | tf_op jit(solution)/shard_map/while/body/eval_jaxpr/ppermute | solution.py:25
  427.2 7.5 %collective-permute-start.2 = (bf16[2,2,32,128,128]{4,3,2,1,0:T(8,128)(2,1)}, bf16[2,2,32,128,128]{4,3,2,1,0:T(8,128)(2,1)}, u32[]{:S(2)}, u32[]{:S(2)}) collective-permute-start(bf16[2,2,32,128,128]{4,3,2,1,0:T(8,128)(2,1)} %fusion), channel_id=1, source_target_pairs={{0,1},{1,0},{2,3},{3,2},{4,5},{5,4},{6,7},{7,6},{8,9},{9,8},{10,11... | collective-permute-start | bytes 12582920 | tf_op jit(solution)/shard_map/ppermute | solution.py:215
  440.7 3.2 copy-start
  444.3 26.2 %collective-permute-start.3 = (bf16[2,32,128,128]{3,2,1,0:T(8,128)(2,1)S(1)}, bf16[2,32,128,128]{3,2,1,0:T(8,128)(2,1)}, u32[]{:S(2)}, u32[]{:S(2)}) collective-permute-start(bf16[2,32,128,128]{3,2,1,0:T(8,128)(2,1)S(1)} %fusion.1), channel_id=1, source_target_pairs={{0,2},{1,5},{2,0},{3,7},{4,6},{5,1},{6,4},{7,3},{8,10},{9,13},{10,... | collective-permute-start | bytes 6291464 | tf_op jit(solution)/shard_map/ppermute | solution.py:215
  476.1 2.0 copy-start.1
  478.2 14.9 %collective-permute-start.4 = (bf16[32,128,128]{2,1,0:T(8,128)(2,1)S(1)}, bf16[32,128,128]{2,1,0:T(8,128)(2,1)S(1)}, u32[]{:S(2)}, u32[]{:S(2)}) collective-permute-start(bf16[32,128,128]{2,1,0:T(8,128)(2,1)S(1)} %fusion.3), channel_id=1, source_target_pairs={{0,4},{1,3},{2,6},{3,1},{4,0},{5,7},{6,2},{7,5},{8,12},{9,11},{10,... | collective-permute-start | bytes 3145736 | tf_op jit(solution)/shard_map/ppermute | solution.py:215
